TPU v7x, 512 devices: a whole 4x8x8 slice. The times are simulated.
512 devices in a mesh: az: 64 (over z, y_lo, core), rad: 8 (over y_hi, x).
Axes of the slice: x: 4, y: 8 (y_hi: 2, y_lo: 4; y = y_hi * 4 + y_lo), z: 8, core: 2. Of those that a mesh axis runs over, the one named last changes fastest.
Arguments:
- density: float32 [1024, 384, 128], P('az', 'rad'), may hold values from 0.5 to 1.5
- flow_vars: float32 [4, 1024, 384, 128], P(None, 'az', 'rad'), may hold values from -6 to 6
- blade_offset: int32 [4], replicated, may hold values from 0 to 4, as said below
- smooth_width: int32 [128], replicated, may hold values from 1 to 4, as said below
Outputs:
- mean_fields: float32 [5, 1024, 384, 128], P(None, 'az', 'rad')
- q_field: float32 [1024, 384, 128], P('az', 'rad')
Inputs may be any that keep to these rules, and one draw needn't show every extreme that they name: `blade_offset`: some blade's passage has the offset 4. `smooth_width`: some axial station uses the half-width 4.
All inputs are finite; a program needn't handle non-finite values.
Results may differ from a plain program's by a relative error of at most 0.00002.
Values sent between devices are 32-bit elements; how exact they have to be, the bound alone decides.
No kernel may reach another device: no remote copies, remote signals or barrier semaphores. Data moves between devices by JAX's collectives and lax.ppermute only.
A program may use at most 64 MiB of HBM per device.

v0:
```python
import math

import jax
import jax.numpy as jnp
from jax import lax
from jax.sharding import PartitionSpec as P

BLADES = 4
MAXOFF = 4
HW = 4


def passed_along(block, axis, distance):
    devices = range(lax.axis_size(axis))
    route = [((i - distance) % len(devices), i) for i in devices]
    return lax.ppermute(block, axis, route)


def extended(block, sides, width, periodic):
    for axis, dim in sides:
        count = lax.axis_size(axis)
        forward = [(i, i + 1) for i in range(count - 1)]
        if periodic:
            forward.append((count - 1, 0))
        backward = [(target, source) for source, target in forward]
        low = lax.ppermute(
            lax.slice_in_dim(block, block.shape[dim] - width, None, axis=dim), axis, forward
        )
        high = lax.ppermute(lax.slice_in_dim(block, 0, width, axis=dim), axis, backward)
        block = jnp.concatenate([low, block, high], axis=dim)
    return block


def smoothing_taps(smooth_width):
    spread = jnp.arange(-HW, HW + 1)
    width = smooth_width.astype(jnp.float32)
    square = (spread.astype(jnp.float32) ** 2)[:, None]
    weights = jnp.where(
        jnp.abs(spread)[:, None] <= smooth_width[None, :],
        jnp.exp(-0.5 * square / (width * width)[None, :]),
        0.0,
    )
    return weights / jnp.sum(weights, axis=0, keepdims=True)


def apply_taps(source, taps, length):
    total = jnp.zeros(source.shape[:1] + (length,) + source.shape[2:], jnp.float32)
    for turn in range(2 * HW + 1):
        total = total + taps[turn] * source[:, turn : turn + length]
    return total


def edge_rate(field, axis):
    count = field.shape[axis]
    upper = jnp.concatenate(
        [
            lax.slice_in_dim(field, 1, count, axis=axis),
            lax.slice_in_dim(field, count - 1, count, axis=axis),
        ],
        axis=axis,
    )
    lower = jnp.concatenate(
        [
            lax.slice_in_dim(field, 0, 1, axis=axis),
            lax.slice_in_dim(field, 0, count - 1, axis=axis),
        ],
        axis=axis,
    )
    places = jnp.arange(count)
    span = jnp.where((places == 0) | (places == count - 1), 1.0, 2.0).astype(field.dtype)
    layout = [1] * field.ndim
    layout[axis] = count
    return (upper - lower) / span.reshape(layout)


def swirl_measure(smoothed, az_rate, radial_rate, axial_rate, radius):
    tensor_aa = radial_rate[0]
    tensor_ab = (az_rate[0] - smoothed[1]) / radius
    tensor_ac = axial_rate[0]
    tensor_ba = radial_rate[1]
    tensor_bb = (az_rate[1] + smoothed[0]) / radius
    tensor_bc = axial_rate[1]
    tensor_ca = radial_rate[2]
    tensor_cb = az_rate[2] / radius
    tensor_cc = axial_rate[2]
    diagonal_part = tensor_aa * tensor_aa + tensor_bb * tensor_bb + tensor_cc * tensor_cc
    cross_part = tensor_ab * tensor_ba + tensor_ac * tensor_ca + tensor_bc * tensor_cb
    return -0.5 * (diagonal_part + 2.0 * cross_part)


def shards(density, flow_vars, blade_offset, smooth_width):
    cells = density.shape[0]
    rad_cells = density.shape[1]
    group = lax.axis_size("az") // BLADES
    place = lax.axis_index("az")
    blade = place // group
    own_offset = jnp.sum(jnp.where(jnp.arange(BLADES) == blade, blade_offset, 0))
    velocity = flow_vars[0:3]
    carried = jnp.concatenate([density[None], density[None] * velocity, flow_vars[3:4]], axis=0)
    ahead = passed_along(carried[:, :MAXOFF], "az", -1)
    contribution = lax.dynamic_slice_in_dim(
        jnp.concatenate([carried, ahead], axis=1), own_offset, cells, 1
    )
    sector_part = contribution
    passing = contribution
    for turn in range(BLADES - 1):
        passing = passed_along(passing, "az", group)
        sector_part = sector_part + passing
    behind = passed_along(sector_part[:, cells - MAXOFF :], "az", 1)
    phase_sums = lax.dynamic_slice_in_dim(
        jnp.concatenate([behind, sector_part], axis=1), MAXOFF - own_offset, cells, 1
    )
    mean_fields = jnp.concatenate(
        [phase_sums[0:1] / BLADES, phase_sums[1:4] / phase_sums[0:1], phase_sums[4:5] / BLADES],
        axis=0,
    )
    fluctuation = velocity - mean_fields[1:4]
    taps = smoothing_taps(smooth_width)
    rimmed = extended(fluctuation, (("az", 1),), HW, True)
    smoothed = apply_taps(rimmed, taps, cells)
    az_side = extended(smoothed, (("az", 1),), 1, True)
    rad_side = extended(smoothed, (("rad", 2),), 1, False)
    dtheta = 2.0 * math.pi / (cells * lax.axis_size("az"))
    az_rate = (az_side[:, 2:] - az_side[:, :-2]) / (2.0 * dtheta)
    total_rad = rad_cells * lax.axis_size("rad")
    rows = lax.axis_index("rad") * rad_cells + jnp.arange(rad_cells)
    upper = jnp.where((rows == total_rad - 1)[:, None], smoothed, rad_side[:, :, 2:])
    lower = jnp.where((rows == 0)[:, None], smoothed, rad_side[:, :, :-2])
    span = jnp.where((rows == 0) | (rows == total_rad - 1), 1.0, 2.0).astype(jnp.float32)
    radial_rate = (upper - lower) / span[:, None]
    axial_rate = edge_rate(smoothed, 3)
    radius = (total_rad / 2 + rows.astype(jnp.float32) + 0.5)[:, None]
    q_field = swirl_measure(smoothed, az_rate, radial_rate, axial_rate, radius)
    return (mean_fields, q_field)


def solution(mesh):
    in_specs = (P("az", "rad", None), P(None, "az", "rad", None), P(), P())
    out_specs = (P(None, "az", "rad", None), P("az", "rad", None))
    return jax.shard_map(shards, mesh=mesh, in_specs=in_specs, out_specs=out_specs, check_vma=False)
```

profile of v0, /device:TPU:6, one launch (start us, length us, event | category | flops | bytes accessed | tf_op | source)
XLA Modules:
  0.0 357.2 jit_solution(11373811175962003650)
XLA Ops:
  1.7 1.5 slice_multiply_fusion
  3.2 13.4 %collective-permute-start = (f32[5,4,48,128]{3,2,1,0:T(8,128)S(1)}, f32[5,4,48,128]{3,2,1,0:T(8,128)S(1)}, u32[]{:S(2)}, u32[]{:S(2)}) collective-permute-start(f32[5,4,48,128]{3,2,1,0:T(8,128)S(1)} %pad_maximum_fusion.7), channel_id=1, source_target_pairs={{8,0},{16,8},{24,16},{32,24},{40,32},{48,40},{56,48},{64,56},{72,6... | collective-permute-start | bytes 1474568 | tf_op jit(solution)/shard_map/ppermute | solution.py:16
  19.3 3.7 %collective-permute-done = f32[5,4,48,128]{3,2,1,0:T(8,128)S(1)} collective-permute-done((f32[5,4,48,128]{3,2,1,0:T(8,128)S(1)}, f32[5,4,48,128]{3,2,1,0:T(8,128)S(1)}, u32[]{:S(2)}, u32[]{:S(2)}) %collective-permute-start) | collective-permute-done | bytes 491552 | tf_op jit(solution)/shard_map/ppermute | solution.py:16
  23.3 1.3 copy-done
  24.6 1.9 collective-permute-start.1
  26.5 42.7 %collective-permute-done.1 = f32[5,16,48,128]{3,2,1,0:T(8,128)S(1)} collective-permute-done((f32[5,16,48,128]{3,2,1,0:T(8,128)S(1)}, f32[5,16,48,128]{3,2,1,0:T(8,128)S(1)}, u32[]{:S(2)}, u32[]{:S(2)}) %collective-permute-start.1) | collective-permute-done | bytes 1966112 | tf_op jit(solution)/shard_map/ppermute | solution.py:16
  69.2 1.3 copy-done.3
  70.5 43.4 %collective-permute-start.2 = (f32[5,16,48,128]{3,2,1,0:T(8,128)S(1)}, f32[5,16,48,128]{3,2,1,0:T(8,128)S(1)}, u32[]{:S(2)}, u32[]{:S(2)}) collective-permute-start(f32[5,16,48,128]{3,2,1,0:T(8,128)S(1)} %collective-permute-done.1), channel_id=1, source_target_pairs={{384,0},{392,8},{400,16},{408,24},{416,32},{424,40},{432,48},{440,... | collective-permute-start | bytes 5898248 | tf_op jit(solution)/shard_map/ppermute | solution.py:16
  113.9 83.6 %collective-permute-done.2 = f32[5,16,48,128]{3,2,1,0:T(8,128)S(1)} collective-permute-done((f32[5,16,48,128]{3,2,1,0:T(8,128)S(1)}, f32[5,16,48,128]{3,2,1,0:T(8,128)S(1)}, u32[]{:S(2)}, u32[]{:S(2)}) %collective-permute-start.2) | collective-permute-done | bytes 1966112 | tf_op jit(solution)/shard_map/ppermute | solution.py:16
  197.5 6.4 %collective-permute-start.3 = (f32[5,16,48,128]{3,2,1,0:T(8,128)S(1)}, f32[5,16,48,128]{3,2,1,0:T(8,128)}, u32[]{:S(2)}, u32[]{:S(2)}) collective-permute-start(f32[5,16,48,128]{3,2,1,0:T(8,128)S(1)} %collective-permute-done.2), channel_id=1, source_target_pairs={{384,0},{392,8},{400,16},{408,24},{416,32},{424,40},{432,48},{440,... | collective-permute-start | bytes 5898248 | tf_op jit(solution)/shard_map/ppermute | solution.py:16
  204.0 92.8 %collective-permute-done.3 = f32[5,16,48,128]{3,2,1,0:T(8,128)} collective-permute-done((f32[5,16,48,128]{3,2,1,0:T(8,128)S(1)}, f32[5,16,48,128]{3,2,1,0:T(8,128)}, u32[]{:S(2)}, u32[]{:S(2)}) %collective-permute-start.3) | collective-permute-done | bytes 1966112 | tf_op jit(solution)/shard_map/ppermute | solution.py:16
  296.8 3.8 %add_add_fusion = f32[5,16,48,128]{3,2,1,0:T(8,128)S(1)} fusion(f32[5,16,48,128]{3,2,1,0:T(8,128)} %collective-permute-done.3, f32[5,16,48,128]{3,2,1,0:T(8,128)} %copy-done.4, f32[5,16,48,128]{3,2,1,0:T(8,128)} %copy-done, f32[5,16,48,128]{3,2,1,0:T(8,128)} %copy-done.3), kind=kLoop, calls=%fused_computation.17 | loop fusion | flops 1474560 | bytes 9830400 | tf_op jit(solution)/shard_map/add | solution.py:108
  300.6 1.9 collective-permute-start.4
  303.9 10.8 %collective-permute-done.4 = f32[5,4,48,128]{3,2,1,0:T(8,128)S(1)} collective-permute-done((f32[5,4,48,128]{3,2,1,0:T(8,128)S(1)}, f32[5,4,48,128]{3,2,1,0:T(8,128)S(1)}, u32[]{:S(2)}, u32[]{:S(2)}) %collective-permute-start.4) | collective-permute-done | bytes 491552 | tf_op jit(solution)/shard_map/ppermute | solution.py:16
  315.1 1.3 copy-done.1
  316.7 1.9 collective-permute-start.5
  318.6 7.5 %collective-permute-start.6 = (f32[3,4,48,128]{3,2,1,0:T(8,128)S(1)}, f32[3,4,48,128]{3,2,1,0:T(8,128)S(1)}, u32[]{:S(2)}, u32[]{:S(2)}) collective-permute-start(f32[3,4,48,128]{3,2,1,0:T(8,128)S(1)} %get-tuple-element.18), channel_id=1, source_target_pairs={{8,0},{16,8},{24,16},{32,24},{40,32},{48,40},{56,48},{64,56},{72,6... | collective-permute-start | bytes 884744 | tf_op jit(solution)/shard_map/ppermute | solution.py:29
  326.2 1.5 pad_maximum_fusion
  328.7 2.0 collective-permute-done.6
  330.7 1.1 fusion.7
  332.7 1.9 collective-permute-start.10
  334.6 7.7 %collective-permute-start.9 = (f32[3,1,48,128]{3,2,1,0:T(8,128)S(1)}, f32[3,1,48,128]{3,2,1,0:T(8,128)S(1)}, u32[]{:S(2)}, u32[]{:S(2)}) collective-permute-start(f32[3,1,48,128]{3,2,1,0:T(8,128)S(1)} %get-tuple-element.15), channel_id=1, source_target_pairs={{8,0},{16,8},{24,16},{32,24},{40,32},{48,40},{56,48},{64,56},{72,6... | collective-permute-start | bytes 221192 | tf_op jit(solution)/shard_map/ppermute | solution.py:29
  342.3 2.7 collective-permute-start.7
  345.1 9.1 %collective-permute-start.8 = (f32[3,16,1,128]{3,2,1,0:T(1,128)S(1)}, f32[3,16,1,128]{3,2,1,0:T(1,128)S(1)}, u32[]{:S(2)}, u32[]{:S(2)}) collective-permute-start(f32[3,16,1,128]{3,2,1,0:T(1,128)S(1)} %get-tuple-element.10), channel_id=1, source_target_pairs={{0,1},{1,2},{2,3},{3,4},{4,5},{5,6},{6,7},{8,9},{9,10},{10,11},{11... | collective-permute-start | bytes 73736 | tf_op jit(solution)/shard_map/ppermute | solution.py:26
  (41 shorter events, 7.7 us)
Async XLA Ops:
  1.7 1.5 copy-start.2
  3.2 13.5 %copy-start.6 = (s32[4]{0:T(128)S(1)}, s32[4]{0:T(128)}, u32[]{:S(2)}) copy-start(s32[4]{0:T(128)} %param.6) | copy-start | bytes 52
  3.2 19.8 %collective-permute-start = (f32[5,4,48,128]{3,2,1,0:T(8,128)S(1)}, f32[5,4,48,128]{3,2,1,0:T(8,128)S(1)}, u32[]{:S(2)}, u32[]{:S(2)}) collective-permute-start(f32[5,4,48,128]{3,2,1,0:T(8,128)S(1)} %pad_maximum_fusion.7), channel_id=1, source_target_pairs={{8,0},{16,8},{24,16},{32,24},{40,32},{48,40},{56,48},{64,56},{72,6... | collective-permute-start | bytes 1474568 | tf_op jit(solution)/shard_map/ppermute | solution.py:16
  19.3 184.6 %copy-start.5 = (s32[128]{0:T(128)S(1)}, s32[128]{0:T(128)}, u32[]{:S(2)}) copy-start(s32[128]{0:T(128)} %param.7) | copy-start | bytes 1540
  23.3 1.3 copy-start
  24.6 44.7 %collective-permute-start.1 = (f32[5,16,48,128]{3,2,1,0:T(8,128)S(1)}, f32[5,16,48,128]{3,2,1,0:T(8,128)S(1)}, u32[]{:S(2)}, u32[]{:S(2)}) collective-permute-start(f32[5,16,48,128]{3,2,1,0:T(8,128)S(1)} %fusion.3), channel_id=1, source_target_pairs={{384,0},{392,8},{400,16},{408,24},{416,32},{424,40},{432,48},{440,... | collective-permute-start | bytes 5898248 | tf_op jit(solution)/shard_map/ppermute | solution.py:16
  69.2 1.3 copy-start.3
  70.5 127.0 %collective-permute-start.2 = (f32[5,16,48,128]{3,2,1,0:T(8,128)S(1)}, f32[5,16,48,128]{3,2,1,0:T(8,128)S(1)}, u32[]{:S(2)}, u32[]{:S(2)}) collective-permute-start(f32[5,16,48,128]{3,2,1,0:T(8,128)S(1)} %collective-permute-done.1), channel_id=1, source_target_pairs={{384,0},{392,8},{400,16},{408,24},{416,32},{424,40},{432,48},{440,... | collective-permute-start | bytes 5898248 | tf_op jit(solution)/shard_map/ppermute | solution.py:16
  197.5 6.5 %copy-start.4 = (f32[5,16,48,128]{3,2,1,0:T(8,128)}, f32[5,16,48,128]{3,2,1,0:T(8,128)S(1)}, u32[]{:S(2)}) copy-start(f32[5,16,48,128]{3,2,1,0:T(8,128)S(1)} %collective-permute-done.2) | copy-start | bytes 5898244
  197.5 99.3 %collective-permute-start.3 = (f32[5,16,48,128]{3,2,1,0:T(8,128)S(1)}, f32[5,16,48,128]{3,2,1,0:T(8,128)}, u32[]{:S(2)}, u32[]{:S(2)}) collective-permute-start(f32[5,16,48,128]{3,2,1,0:T(8,128)S(1)} %collective-permute-done.2), channel_id=1, source_target_pairs={{384,0},{392,8},{400,16},{408,24},{416,32},{424,40},{432,48},{440,... | collective-permute-start | bytes 5898248 | tf_op jit(solution)/shard_map/ppermute | solution.py:16
  300.6 14.2 %collective-permute-start.4 = (f32[5,4,48,128]{3,2,1,0:T(8,128)S(1)}, f32[5,4,48,128]{3,2,1,0:T(8,128)S(1)}, u32[]{:S(2)}, u32[]{:S(2)}) collective-permute-start(f32[5,4,48,128]{3,2,1,0:T(8,128)S(1)} %slice.209), channel_id=1, source_target_pairs={{504,0},{0,8},{8,16},{16,24},{24,32},{32,40},{40,48},{48,56},{56,6... | collective-permute-start | bytes 1474568 | tf_op jit(solution)/shard_map/ppermute | solution.py:16
  315.0 1.4 copy-start.1
  316.7 12.0 %collective-permute-start.5 = (f32[3,4,48,128]{3,2,1,0:T(8,128)S(1)}, f32[3,4,48,128]{3,2,1,0:T(8,128)S(1)}, u32[]{:S(2)}, u32[]{:S(2)}) collective-permute-start(f32[3,4,48,128]{3,2,1,0:T(8,128)S(1)} %get-tuple-element.17), channel_id=1, source_target_pairs={{0,8},{8,16},{16,24},{24,32},{32,40},{40,48},{48,56},{56,64},{64,7... | collective-permute-start | bytes 884744 | tf_op jit(solution)/shard_map/ppermute | solution.py:26
  318.6 12.1 %collective-permute-start.6 = (f32[3,4,48,128]{3,2,1,0:T(8,128)S(1)}, f32[3,4,48,128]{3,2,1,0:T(8,128)S(1)}, u32[]{:S(2)}, u32[]{:S(2)}) collective-permute-start(f32[3,4,48,128]{3,2,1,0:T(8,128)S(1)} %get-tuple-element.18), channel_id=1, source_target_pairs={{8,0},{16,8},{24,16},{32,24},{40,32},{48,40},{56,48},{64,56},{72,6... | collective-permute-start | bytes 884744 | tf_op jit(solution)/shard_map/ppermute | solution.py:29
  332.7 23.0 %collective-permute-start.10 = (f32[3,1,48,128]{3,2,1,0:T(8,128)S(1)}, f32[3,1,48,128]{3,2,1,0:T(8,128)S(1)}, u32[]{:S(2)}, u32[]{:S(2)}) collective-permute-start(f32[3,1,48,128]{3,2,1,0:T(8,128)S(1)} %get-tuple-element.16), channel_id=1, source_target_pairs={{0,8},{8,16},{16,24},{24,32},{32,40},{40,48},{48,56},{56,64},{64,7... | collective-permute-start | bytes 221192 | tf_op jit(solution)/shard_map/ppermute | solution.py:26
  334.6 21.1 %collective-permute-start.9 = (f32[3,1,48,128]{3,2,1,0:T(8,128)S(1)}, f32[3,1,48,128]{3,2,1,0:T(8,128)S(1)}, u32[]{:S(2)}, u32[]{:S(2)}) collective-permute-start(f32[3,1,48,128]{3,2,1,0:T(8,128)S(1)} %get-tuple-element.15), channel_id=1, source_target_pairs={{8,0},{16,8},{24,16},{32,24},{40,32},{48,40},{56,48},{64,56},{72,6... | collective-permute-start | bytes 221192 | tf_op jit(solution)/shard_map/ppermute | solution.py:29
  342.3 12.6 %collective-permute-start.7 = (f32[3,16,1,128]{3,2,1,0:T(1,128)S(1)}, f32[3,16,1,128]{3,2,1,0:T(1,128)S(1)}, u32[]{:S(2)}, u32[]{:S(2)}) collective-permute-start(f32[3,16,1,128]{3,2,1,0:T(1,128)S(1)} %get-tuple-element.9), channel_id=1, source_target_pairs={{1,0},{2,1},{3,2},{4,3},{5,4},{6,5},{7,6},{9,8},{10,9},{11,10},{12... | collective-permute-start | bytes 73736 | tf_op jit(solution)/shard_map/ppermute | solution.py:29
  345.1 10.6 %collective-permute-start.8 = (f32[3,16,1,128]{3,2,1,0:T(1,128)S(1)}, f32[3,16,1,128]{3,2,1,0:T(1,128)S(1)}, u32[]{:S(2)}, u32[]{:S(2)}) collective-permute-start(f32[3,16,1,128]{3,2,1,0:T(1,128)S(1)} %get-tuple-element.10), channel_id=1, source_target_pairs={{0,1},{1,2},{2,3},{3,4},{4,5},{5,6},{6,7},{8,9},{9,10},{10,11},{11... | collective-permute-start | bytes 73736 | tf_op jit(solution)/shard_map/ppermute | solution.py:26
where the time goes:
time: 360 us; the launch traced here: 357 us
  waiting for transfers between devices  238 us (66%)
  starting transfers between devices  98 us (27%)
  other arithmetic  11.8 us (3%)
  local copies, waits for them, and re-layouts  5.79 us (2%)
  between operations  4.21 us (1%)
    ppermute x5, waiting for transfers between devices, passed_along(): return lax.ppermute(block, axis, route)  234 us
    ppermute x5, starting transfers between devices, passed_along(): return lax.ppermute(block, axis, route)  67 us
    ppermute x3, starting transfers between devices, extended(): lax.ppermute(lax.slice_in_dim(block, 0, width, axis=dim), axis, backward)  18 us
    ppermute x3, starting transfers between devices, extended(): lax.ppermute(lax.slice_in_dim(block, block.shape[dim] - width, None, axis...  13 us
  transfers between devices with their start and end apart: 11, of which 8 were waited for; matrix products, arithmetic and copies ran while one was open for 1% of the time, Pallas kernels for 0%

commit v1 on v0

--- a/solution.py
+++ b/solution.py
@@ -8,6 +8,7 @@
 BLADES = 4
 MAXOFF = 4
 HW = 4
+AZ = ("blade", "slab")
 
 
 def passed_along(block, axis, distance):
@@ -91,22 +92,17 @@
 def shards(density, flow_vars, blade_offset, smooth_width):
     cells = density.shape[0]
     rad_cells = density.shape[1]
-    group = lax.axis_size("az") // BLADES
-    place = lax.axis_index("az")
-    blade = place // group
+    group = lax.axis_size("slab")
+    blade = lax.axis_index("blade")
     own_offset = jnp.sum(jnp.where(jnp.arange(BLADES) == blade, blade_offset, 0))
     velocity = flow_vars[0:3]
     carried = jnp.concatenate([density[None], density[None] * velocity, flow_vars[3:4]], axis=0)
-    ahead = passed_along(carried[:, :MAXOFF], "az", -1)
+    ahead = passed_along(carried[:, :MAXOFF], AZ, -1)
     contribution = lax.dynamic_slice_in_dim(
         jnp.concatenate([carried, ahead], axis=1), own_offset, cells, 1
     )
-    sector_part = contribution
-    passing = contribution
-    for turn in range(BLADES - 1):
-        passing = passed_along(passing, "az", group)
-        sector_part = sector_part + passing
-    behind = passed_along(sector_part[:, cells - MAXOFF :], "az", 1)
+    sector_part = lax.psum(contribution, "blade")
+    behind = passed_along(sector_part[:, cells - MAXOFF :], AZ, 1)
     phase_sums = lax.dynamic_slice_in_dim(
         jnp.concatenate([behind, sector_part], axis=1), MAXOFF - own_offset, cells, 1
     )
@@ -116,11 +112,11 @@
     )
     fluctuation = velocity - mean_fields[1:4]
     taps = smoothing_taps(smooth_width)
-    rimmed = extended(fluctuation, (("az", 1),), HW, True)
+    rimmed = extended(fluctuation, ((AZ, 1),), HW, True)
     smoothed = apply_taps(rimmed, taps, cells)
-    az_side = extended(smoothed, (("az", 1),), 1, True)
+    az_side = extended(smoothed, ((AZ, 1),), 1, True)
     rad_side = extended(smoothed, (("rad", 2),), 1, False)
-    dtheta = 2.0 * math.pi / (cells * lax.axis_size("az"))
+    dtheta = 2.0 * math.pi / (cells * lax.axis_size(AZ))
     az_rate = (az_side[:, 2:] - az_side[:, :-2]) / (2.0 * dtheta)
     total_rad = rad_cells * lax.axis_size("rad")
     rows = lax.axis_index("rad") * rad_cells + jnp.arange(rad_cells)
@@ -135,6 +131,8 @@
 
 
 def solution(mesh):
-    in_specs = (P("az", "rad", None), P(None, "az", "rad", None), P(), P())
-    out_specs = (P(None, "az", "rad", None), P("az", "rad", None))
-    return jax.shard_map(shards, mesh=mesh, in_specs=in_specs, out_specs=out_specs, check_vma=False)
+    az, rad = mesh.devices.shape
+    split = jax.sharding.Mesh(mesh.devices.reshape(BLADES, az // BLADES, rad), ("blade", "slab", "rad"))
+    in_specs = (P(AZ, "rad", None), P(None, AZ, "rad", None), P(), P())
+    out_specs = (P(None, AZ, "rad", None), P(AZ, "rad", None))
+    return jax.shard_map(shards, mesh=split, in_specs=in_specs, out_specs=out_specs, check_vma=False)

time: 360 us -> 196 us (0.54)
  waiting for transfers between devices: 238 us -> 115 us
  starting transfers between devices: 98 us -> 45 us
  between operations: 4.21 us -> 17.5 us
    ppermute x5 -> x2, waiting for transfers between devices: 234 us -> 14.5 us  [passed_along(): return lax.ppermute(block, axis, route)]
    psum x0 -> x1, waiting for transfers between devices: none -> 95.6 us  [shards(): sector_part = lax.psum(contribution, 'blade')]
    ppermute x5 -> x2, starting transfers between devices: 67 us -> 15.3 us  [passed_along(): return lax.ppermute(block, axis, route)]
    add x1 -> x0, other arithmetic: 3.79 us -> none  [shards(): sector_part = sector_part + passing]
  transfers between devices with their start and end apart: 11 -> 9, of which waited for: 8 -> 5; matrix products, arithmetic and copies ran while one was open for 1% -> 2% of each run, Pallas kernels for 0% -> 0%
where the time goes in v1:
time: 196 us; the launch traced here: 193 us
  waiting for transfers between devices  115 us (59%)
  starting transfers between devices  45 us (23%)
  between operations  17.5 us (9%)
  other arithmetic  10.7 us (5%)
  local copies, waits for them, and re-layouts  4.86 us (2%)
    psum x1, waiting for transfers between devices, shards(): sector_part = lax.psum(contribution, 'blade')  95.6 us
    ppermute x3, starting transfers between devices, extended(): lax.ppermute(lax.slice_in_dim(block, 0, width, axis=dim), axis, backward)  16.6 us
    ppermute x2, starting transfers between devices, passed_along(): return lax.ppermute(block, axis, route)  15.3 us
    ppermute x2, waiting for transfers between devices, passed_along(): return lax.ppermute(block, axis, route)  14.5 us
    ppermute x3, starting transfers between devices, extended(): lax.ppermute(lax.slice_in_dim(block, block.shape[dim] - width, None, axis...  12.9 us
    ppermute x3, waiting for transfers between devices, extended(): lax.ppermute(lax.slice_in_dim(block, block.shape[dim] - width, None, axis...  4.92 us
  transfers between devices with their start and end apart: 9, of which 5 were waited for; matrix products, arithmetic and copies ran while one was open for 2% of the time, Pallas kernels for 0%

profile of v1, /device:TPU:6, one launch (start us, length us, event | category | flops | bytes accessed | tf_op | source)
XLA Modules:
  0.0 193.0 jit_solution(17805172556178679589)
XLA Ops:
  7.2 1.0 slice.161
  8.2 1.5 slice_multiply_fusion
  9.8 13.4 %collective-permute-start = (f32[5,4,48,128]{3,2,1,0:T(8,128)S(1)}, f32[5,4,48,128]{3,2,1,0:T(8,128)S(1)}, u32[]{:S(2)}, u32[]{:S(2)}) collective-permute-start(f32[5,4,48,128]{3,2,1,0:T(8,128)S(1)} %pad_maximum_fusion.7), channel_id=1, source_target_pairs={{8,0},{16,8},{24,16},{32,24},{40,32},{48,40},{56,48},{64,56},{72,6... | collective-permute-start | bytes 1474568 | tf_op jit(solution)/shard_map/ppermute | solution.py:17
  23.3 0.6 fusion.54
  25.8 3.7 %collective-permute-done = f32[5,4,48,128]{3,2,1,0:T(8,128)S(1)} collective-permute-done((f32[5,4,48,128]{3,2,1,0:T(8,128)S(1)}, f32[5,4,48,128]{3,2,1,0:T(8,128)S(1)}, u32[]{:S(2)}, u32[]{:S(2)}) %collective-permute-start) | collective-permute-done | bytes 491552 | tf_op jit(solution)/shard_map/ppermute | solution.py:17
  29.6 1.5 fusion.3
  31.9 95.6 %all-reduce.2.cloned.1.call-done = f32[5,16,48,128]{3,2,1,0:T(8,128)} async-done(((f32[5,16,48,128]{3,2,1,0:T(8,128)}), f32[5,16,48,128]{3,2,1,0:T(8,128)}) %all-reduce.2.cloned.1.call-update) | async-done | bytes 1966096 | tf_op jit(solution)/shard_map/psum | solution.py:104
  127.4 1.1 slice.209
  128.5 1.9 collective-permute-start.1
  131.8 10.7 %collective-permute-done.1 = f32[5,4,48,128]{3,2,1,0:T(8,128)S(1)} collective-permute-done((f32[5,4,48,128]{3,2,1,0:T(8,128)S(1)}, f32[5,4,48,128]{3,2,1,0:T(8,128)S(1)}, u32[]{:S(2)}, u32[]{:S(2)}) %collective-permute-start.1) | collective-permute-done | bytes 491552 | tf_op jit(solution)/shard_map/ppermute | solution.py:17
  142.6 1.7 fusion
  144.3 1.3 copy-done
  145.9 1.9 collective-permute-start.2
  147.9 7.5 %collective-permute-start.3 = (f32[3,4,48,128]{3,2,1,0:T(8,128)S(1)}, f32[3,4,48,128]{3,2,1,0:T(8,128)S(1)}, u32[]{:S(2)}, u32[]{:S(2)}) collective-permute-start(f32[3,4,48,128]{3,2,1,0:T(8,128)S(1)} %get-tuple-element.18), channel_id=1, source_target_pairs={{8,0},{16,8},{24,16},{32,24},{40,32},{48,40},{56,48},{64,56},{72,6... | collective-permute-start | bytes 884744 | tf_op jit(solution)/shard_map/ppermute | solution.py:30
  155.4 1.5 pad_maximum_fusion
  156.9 4.1 %collective-permute-done.2 = f32[3,4,48,128]{3,2,1,0:T(8,128)S(1)} collective-permute-done((f32[3,4,48,128]{3,2,1,0:T(8,128)S(1)}, f32[3,4,48,128]{3,2,1,0:T(8,128)S(1)}, u32[]{:S(2)}, u32[]{:S(2)}) %collective-permute-start.2) | collective-permute-done | bytes 294944 | tf_op jit(solution)/shard_map/ppermute | solution.py:27
  161.0 1.1 fusion.7
  163.0 6.3 %collective-permute-start.6 = (f32[3,1,48,128]{3,2,1,0:T(8,128)S(1)}, f32[3,1,48,128]{3,2,1,0:T(8,128)S(1)}, u32[]{:S(2)}, u32[]{:S(2)}) collective-permute-start(f32[3,1,48,128]{3,2,1,0:T(8,128)S(1)} %get-tuple-element.15), channel_id=1, source_target_pairs={{8,0},{16,8},{24,16},{32,24},{40,32},{48,40},{56,48},{64,56},{72,6... | collective-permute-start | bytes 221192 | tf_op jit(solution)/shard_map/ppermute | solution.py:30
  169.3 1.9 collective-permute-start.7
  171.2 2.8 %collective-permute-start.4 = (f32[3,16,1,128]{3,2,1,0:T(1,128)S(1)}, f32[3,16,1,128]{3,2,1,0:T(1,128)S(1)}, u32[]{:S(2)}, u32[]{:S(2)}) collective-permute-start(f32[3,16,1,128]{3,2,1,0:T(1,128)S(1)} %get-tuple-element.9), channel_id=1, source_target_pairs={{1,0},{2,1},{3,2},{4,3},{5,4},{6,5},{7,6},{9,8},{10,9},{11,10},{12... | collective-permute-start | bytes 73736 | tf_op jit(solution)/shard_map/ppermute | solution.py:30
  174.0 9.1 %collective-permute-start.5 = (f32[3,16,1,128]{3,2,1,0:T(1,128)S(1)}, f32[3,16,1,128]{3,2,1,0:T(1,128)S(1)}, u32[]{:S(2)}, u32[]{:S(2)}) collective-permute-start(f32[3,16,1,128]{3,2,1,0:T(1,128)S(1)} %get-tuple-element.10), channel_id=1, source_target_pairs={{0,1},{1,2},{2,3},{3,4},{4,5},{5,6},{6,7},{8,9},{9,10},{10,11},{11... | collective-permute-start | bytes 73736 | tf_op jit(solution)/shard_map/ppermute | solution.py:27
  183.1 0.7 fusion.32
  183.8 0.8 collective-permute-done.5
  185.1 1.1 fusion.38
  (31 shorter events, 2.6 us)
Async XLA Ops:
  7.2 120.3 %all-reduce.2.cloned.1.call-start = ((), (), s32[]{:S(2)}) async-start(), calls=%async_computation | async-start | bytes 3932160 | tf_op jit(solution)/shard_map/psum | solution.py:104
  8.2 1.5 copy-start.1
  9.8 13.5 %copy-start.3 = (s32[4]{0:T(128)S(1)}, s32[4]{0:T(128)}, u32[]{:S(2)}) copy-start(s32[4]{0:T(128)} %param.6) | copy-start | bytes 52
  9.8 19.8 %collective-permute-start = (f32[5,4,48,128]{3,2,1,0:T(8,128)S(1)}, f32[5,4,48,128]{3,2,1,0:T(8,128)S(1)}, u32[]{:S(2)}, u32[]{:S(2)}) collective-permute-start(f32[5,4,48,128]{3,2,1,0:T(8,128)S(1)} %pad_maximum_fusion.7), channel_id=1, source_target_pairs={{8,0},{16,8},{24,16},{32,24},{40,32},{48,40},{56,48},{64,56},{72,6... | collective-permute-start | bytes 1474568 | tf_op jit(solution)/shard_map/ppermute | solution.py:17
  31.1 0.7 copy-start.2
  128.5 14.1 %collective-permute-start.1 = (f32[5,4,48,128]{3,2,1,0:T(8,128)S(1)}, f32[5,4,48,128]{3,2,1,0:T(8,128)S(1)}, u32[]{:S(2)}, u32[]{:S(2)}) collective-permute-start(f32[5,4,48,128]{3,2,1,0:T(8,128)S(1)} %slice.209), channel_id=1, source_target_pairs={{504,0},{0,8},{8,16},{16,24},{24,32},{32,40},{40,48},{48,56},{56,6... | collective-permute-start | bytes 1474568 | tf_op jit(solution)/shard_map/ppermute | solution.py:17
  144.2 1.4 copy-start
  145.9 15.1 %collective-permute-start.2 = (f32[3,4,48,128]{3,2,1,0:T(8,128)S(1)}, f32[3,4,48,128]{3,2,1,0:T(8,128)S(1)}, u32[]{:S(2)}, u32[]{:S(2)}) collective-permute-start(f32[3,4,48,128]{3,2,1,0:T(8,128)S(1)} %get-tuple-element.17), channel_id=1, source_target_pairs={{0,8},{8,16},{16,24},{24,32},{32,40},{40,48},{48,56},{56,64},{64,7... | collective-permute-start | bytes 884744 | tf_op jit(solution)/shard_map/ppermute | solution.py:27
  147.9 13.2 %collective-permute-start.3 = (f32[3,4,48,128]{3,2,1,0:T(8,128)S(1)}, f32[3,4,48,128]{3,2,1,0:T(8,128)S(1)}, u32[]{:S(2)}, u32[]{:S(2)}) collective-permute-start(f32[3,4,48,128]{3,2,1,0:T(8,128)S(1)} %get-tuple-element.18), channel_id=1, source_target_pairs={{8,0},{16,8},{24,16},{32,24},{40,32},{48,40},{56,48},{64,56},{72,6... | collective-permute-start | bytes 884744 | tf_op jit(solution)/shard_map/ppermute | solution.py:30
  163.0 21.7 %collective-permute-start.6 = (f32[3,1,48,128]{3,2,1,0:T(8,128)S(1)}, f32[3,1,48,128]{3,2,1,0:T(8,128)S(1)}, u32[]{:S(2)}, u32[]{:S(2)}) collective-permute-start(f32[3,1,48,128]{3,2,1,0:T(8,128)S(1)} %get-tuple-element.15), channel_id=1, source_target_pairs={{8,0},{16,8},{24,16},{32,24},{40,32},{48,40},{56,48},{64,56},{72,6... | collective-permute-start | bytes 221192 | tf_op jit(solution)/shard_map/ppermute | solution.py:30
  169.3 15.3 %collective-permute-start.7 = (f32[3,1,48,128]{3,2,1,0:T(8,128)S(1)}, f32[3,1,48,128]{3,2,1,0:T(8,128)S(1)}, u32[]{:S(2)}, u32[]{:S(2)}) collective-permute-start(f32[3,1,48,128]{3,2,1,0:T(8,128)S(1)} %get-tuple-element.16), channel_id=1, source_target_pairs={{0,8},{8,16},{16,24},{24,32},{32,40},{40,48},{48,56},{56,64},{64,7... | collective-permute-start | bytes 221192 | tf_op jit(solution)/shard_map/ppermute | solution.py:27
  171.2 12.6 %collective-permute-start.4 = (f32[3,16,1,128]{3,2,1,0:T(1,128)S(1)}, f32[3,16,1,128]{3,2,1,0:T(1,128)S(1)}, u32[]{:S(2)}, u32[]{:S(2)}) collective-permute-start(f32[3,16,1,128]{3,2,1,0:T(1,128)S(1)} %get-tuple-element.9), channel_id=1, source_target_pairs={{1,0},{2,1},{3,2},{4,3},{5,4},{6,5},{7,6},{9,8},{10,9},{11,10},{12... | collective-permute-start | bytes 73736 | tf_op jit(solution)/shard_map/ppermute | solution.py:30
  174.0 10.6 %collective-permute-start.5 = (f32[3,16,1,128]{3,2,1,0:T(1,128)S(1)}, f32[3,16,1,128]{3,2,1,0:T(1,128)S(1)}, u32[]{:S(2)}, u32[]{:S(2)}) collective-permute-start(f32[3,16,1,128]{3,2,1,0:T(1,128)S(1)} %get-tuple-element.10), channel_id=1, source_target_pairs={{0,1},{1,2},{2,3},{3,4},{4,5},{5,6},{6,7},{8,9},{9,10},{10,11},{11... | collective-permute-start | bytes 73736 | tf_op jit(solution)/shard_map/ppermute | solution.py:27
Sparse Core Ops, SparseCore 0:
  31.3 96.1 all-reduce.1

commit v2 on v1

--- a/solution.py
+++ b/solution.py
@@ -30,6 +30,35 @@
         high = lax.ppermute(lax.slice_in_dim(block, 0, width, axis=dim), axis, backward)
         block = jnp.concatenate([low, block, high], axis=dim)
     return block
+
+
+def ring_half(block, step):
+    count = lax.axis_size("blade")
+    place = lax.axis_index("blade")
+    route = [(i, (i + step) % count) for i in range(count)]
+    width = block.shape[1] // count
+    doubled = jnp.concatenate([block, block], axis=1)
+
+    def piece(index):
+        return lax.dynamic_slice_in_dim(doubled, index * width, width, 1)
+
+    total = piece(place % count)
+    for turn in range(1, count):
+        total = lax.ppermute(total, "blade", route) + piece((place - step * turn) % count)
+    pieces = [total]
+    for turn in range(1, count):
+        pieces.append(lax.ppermute(pieces[-1], "blade", route))
+    if step > 0:
+        sequence, first = pieces[::-1], (place - 2) % count
+    else:
+        sequence, first = pieces, (place - 1) % count
+    ordered = jnp.concatenate(sequence * 2, axis=1)
+    return lax.dynamic_slice_in_dim(ordered, ((count - first) % count) * width, block.shape[1], 1)
+
+
+def ring_sum(block):
+    half = block.shape[1] // 2
+    return jnp.concatenate([ring_half(block[:, :half], 1), ring_half(block[:, half:], -1)], axis=1)
 
 
 def smoothing_taps(smooth_width):
@@ -101,7 +130,7 @@
     contribution = lax.dynamic_slice_in_dim(
         jnp.concatenate([carried, ahead], axis=1), own_offset, cells, 1
     )
-    sector_part = lax.psum(contribution, "blade")
+    sector_part = ring_sum(contribution)
     behind = passed_along(sector_part[:, cells - MAXOFF :], AZ, 1)
     phase_sums = lax.dynamic_slice_in_dim(
         jnp.concatenate([behind, sector_part], axis=1), MAXOFF - own_offset, cells, 1

time: 196 us -> 182 us (0.929)
  the two profiles are of different devices: /device:TPU:6 before, /device:TPU:121 now
where the time goes in v2:
time: 182 us; the launch traced here: 181 us
  starting transfers between devices  84.5 us (46%)
  waiting for transfers between devices  73.3 us (40%)
  local copies, waits for them, and re-layouts  9.89 us (5%)
  other arithmetic  9.27 us (5%)
  between operations  4.59 us (3%)
    ppermute x6, waiting for transfers between devices, ring_half(): pieces.append(lax.ppermute(pieces[-1], 'blade', route))  28.1 us
    ppermute x6, starting transfers between devices, ring_half(): lax.ppermute(total, 'blade', route) + piece((place - step * turn) % count)  26.7 us
    ppermute x6, starting transfers between devices, ring_half(): pieces.append(lax.ppermute(pieces[-1], 'blade', route))  21.6 us
    ppermute x6, waiting for transfers between devices, ring_half(): lax.ppermute(total, 'blade', route) + piece((place - step * turn) % count)  17.7 us
    ppermute x3, starting transfers between devices, extended(): lax.ppermute(lax.slice_in_dim(block, block.shape[dim] - width, None, axis...  16.8 us
    ppermute x2, waiting for transfers between devices, passed_along(): return lax.ppermute(block, axis, route)  13.7 us
    ppermute x2, starting transfers between devices, passed_along(): return lax.ppermute(block, axis, route)  13.6 us
    ppermute x3, waiting for transfers between devices, extended(): lax.ppermute(lax.slice_in_dim(block, block.shape[dim] - width, None, axis...  7.4 us
  transfers between devices with their start and end apart: 20, of which 14 were waited for; matrix products, arithmetic and copies ran while one was open for 3% of the time, Pallas kernels for 0%

profile of v2, /device:TPU:121, one launch (start us, length us, event | category | flops | bytes accessed | tf_op | source)
XLA Modules:
  0.0 181.5 jit_solution(4486523048428454290)
XLA Ops:
  3.2 2.6 %collective-permute-start = (f32[5,4,48,128]{3,2,1,0:T(8,128)S(1)}, f32[5,4,48,128]{3,2,1,0:T(8,128)S(1)}, u32[]{:S(2)}, u32[]{:S(2)}) collective-permute-start(f32[5,4,48,128]{3,2,1,0:T(8,128)S(1)} %pad_maximum_fusion.7), channel_id=1, source_target_pairs={{8,0},{16,8},{24,16},{32,24},{40,32},{48,40},{56,48},{64,56},{72,6... | collective-permute-start | bytes 1474568 | tf_op jit(solution)/shard_map/ppermute | solution.py:17
  8.4 8.2 %collective-permute-done = f32[5,4,48,128]{3,2,1,0:T(8,128)S(1)} collective-permute-done((f32[5,4,48,128]{3,2,1,0:T(8,128)S(1)}, f32[5,4,48,128]{3,2,1,0:T(8,128)S(1)}, u32[]{:S(2)}, u32[]{:S(2)}) %collective-permute-start) | collective-permute-done | bytes 491552 | tf_op jit(solution)/shard_map/ppermute | solution.py:17
  17.2 7.0 %collective-permute-start.8 = (f32[5,2,48,128]{3,2,1,0:T(8,128)S(1)}, f32[5,2,48,128]{3,2,1,0:T(8,128)S(1)}, u32[]{:S(2)}, u32[]{:S(2)}) collective-permute-start(f32[5,2,48,128]{3,2,1,0:T(8,128)S(1)} %fusion.54), channel_id=1, source_target_pairs={{0,128},{128,256},{256,384},{384,0},{1,129},{129,257},{257,385},{3... | collective-permute-start | bytes 737288 | tf_op jit(solution)/shard_map/ppermute | solution.py:47
  24.3 5.3 %collective-permute-start.1 = (f32[5,2,48,128]{3,2,1,0:T(8,128)S(1)}, f32[5,2,48,128]{3,2,1,0:T(8,128)S(1)}, u32[]{:S(2)}, u32[]{:S(2)}) collective-permute-start(f32[5,2,48,128]{3,2,1,0:T(8,128)S(1)} %fusion.61), channel_id=1, source_target_pairs={{0,384},{128,0},{256,128},{384,256},{1,385},{129,1},{257,129},{385... | collective-permute-start | bytes 737288 | tf_op jit(solution)/shard_map/ppermute | solution.py:47
  29.7 5.3 %collective-permute-done.8 = f32[5,2,48,128]{3,2,1,0:T(8,128)S(1)} collective-permute-done((f32[5,2,48,128]{3,2,1,0:T(8,128)S(1)}, f32[5,2,48,128]{3,2,1,0:T(8,128)S(1)}, u32[]{:S(2)}, u32[]{:S(2)}) %collective-permute-start.8) | collective-permute-done | bytes 245792 | tf_op jit(solution)/shard_map/ppermute | solution.py:47
  37.1 5.4 %collective-permute-start.2 = (f32[5,2,48,128]{3,2,1,0:T(8,128)S(1)}, f32[5,2,48,128]{3,2,1,0:T(8,128)S(1)}, u32[]{:S(2)}, u32[]{:S(2)}) collective-permute-start(f32[5,2,48,128]{3,2,1,0:T(8,128)S(1)} %fusion.63), channel_id=1, source_target_pairs={{0,384},{128,0},{256,128},{384,256},{1,385},{129,1},{257,129},{385... | collective-permute-start | bytes 737288 | tf_op jit(solution)/shard_map/ppermute | solution.py:47
  42.6 6.0 %collective-permute-done.9 = f32[5,2,48,128]{3,2,1,0:T(8,128)S(1)} collective-permute-done((f32[5,2,48,128]{3,2,1,0:T(8,128)S(1)}, f32[5,2,48,128]{3,2,1,0:T(8,128)S(1)}, u32[]{:S(2)}, u32[]{:S(2)}) %collective-permute-start.9) | collective-permute-done | bytes 245792 | tf_op jit(solution)/shard_map/ppermute | solution.py:47
  50.6 2.2 %collective-permute-done.2 = f32[5,2,48,128]{3,2,1,0:T(8,128)S(1)} collective-permute-done((f32[5,2,48,128]{3,2,1,0:T(8,128)S(1)}, f32[5,2,48,128]{3,2,1,0:T(8,128)S(1)}, u32[]{:S(2)}, u32[]{:S(2)}) %collective-permute-start.2) | collective-permute-done | bytes 245792 | tf_op jit(solution)/shard_map/ppermute | solution.py:47
  52.9 5.1 %collective-permute-start.3 = (f32[5,2,48,128]{3,2,1,0:T(8,128)S(1)}, f32[5,2,48,128]{3,2,1,0:T(8,128)S(1)}, u32[]{:S(2)}, u32[]{:S(2)}) collective-permute-start(f32[5,2,48,128]{3,2,1,0:T(8,128)S(1)} %fusion.65), channel_id=1, source_target_pairs={{0,384},{128,0},{256,128},{384,256},{1,385},{129,1},{257,129},{385... | collective-permute-start | bytes 737288 | tf_op jit(solution)/shard_map/ppermute | solution.py:47
  58.0 4.1 %collective-permute-done.10 = f32[5,2,48,128]{3,2,1,0:T(8,128)S(1)} collective-permute-done((f32[5,2,48,128]{3,2,1,0:T(8,128)S(1)}, f32[5,2,48,128]{3,2,1,0:T(8,128)S(1)}, u32[]{:S(2)}, u32[]{:S(2)}) %collective-permute-start.10) | collective-permute-done | bytes 245792 | tf_op jit(solution)/shard_map/ppermute | solution.py:47
  64.9 5.5 %collective-permute-start.4 = (f32[5,2,48,128]{3,2,1,0:T(8,128)S(1)}, f32[5,2,48,128]{3,2,1,0:T(8,128)S(1)}, u32[]{:S(2)}, u32[]{:S(2)}) collective-permute-start(f32[5,2,48,128]{3,2,1,0:T(8,128)S(1)} %get-tuple-element.5), channel_id=1, source_target_pairs={{0,384},{128,0},{256,128},{384,256},{1,385},{129,1},{257,129},{385... | collective-permute-start | bytes 737288 | tf_op jit(solution)/shard_map/ppermute | solution.py:50
  70.5 8.0 %collective-permute-done.11 = f32[5,2,48,128]{3,2,1,0:T(8,128)S(1)} collective-permute-done((f32[5,2,48,128]{3,2,1,0:T(8,128)S(1)}, f32[5,2,48,128]{3,2,1,0:T(8,128)S(1)}, u32[]{:S(2)}, u32[]{:S(2)}) %collective-permute-start.11) | collective-permute-done | bytes 245792 | tf_op jit(solution)/shard_map/ppermute | solution.py:50
  81.0 4.9 %collective-permute-start.5 = (f32[5,2,48,128]{3,2,1,0:T(8,128)S(1)}, f32[5,2,48,128]{3,2,1,0:T(8,128)S(1)}, u32[]{:S(2)}, u32[]{:S(2)}) collective-permute-start(f32[5,2,48,128]{3,2,1,0:T(8,128)S(1)} %collective-permute-done.4), channel_id=1, source_target_pairs={{0,384},{128,0},{256,128},{384,256},{1,385},{129,1},{257,129},{385... | collective-permute-start | bytes 737288 | tf_op jit(solution)/shard_map/ppermute | solution.py:50
  86.0 8.0 %collective-permute-done.12 = f32[5,2,48,128]{3,2,1,0:T(8,128)S(1)} collective-permute-done((f32[5,2,48,128]{3,2,1,0:T(8,128)S(1)}, f32[5,2,48,128]{3,2,1,0:T(8,128)S(1)}, u32[]{:S(2)}, u32[]{:S(2)}) %collective-permute-start.12) | collective-permute-done | bytes 245792 | tf_op jit(solution)/shard_map/ppermute | solution.py:50
  98.0 5.5 %collective-permute-start.6 = (f32[5,2,48,128]{3,2,1,0:T(8,128)S(1)}, f32[5,2,48,128]{3,2,1,0:T(8,128)S(1)}, u32[]{:S(2)}, u32[]{:S(2)}) collective-permute-start(f32[5,2,48,128]{3,2,1,0:T(8,128)S(1)} %collective-permute-done.5), channel_id=1, source_target_pairs={{0,384},{128,0},{256,128},{384,256},{1,385},{129,1},{257,129},{385... | collective-permute-start | bytes 737288 | tf_op jit(solution)/shard_map/ppermute | solution.py:50
  104.2 2.4 %collective-permute-done.13 = f32[5,2,48,128]{3,2,1,0:T(8,128)S(1)} collective-permute-done((f32[5,2,48,128]{3,2,1,0:T(8,128)S(1)}, f32[5,2,48,128]{3,2,1,0:T(8,128)S(1)}, u32[]{:S(2)}, u32[]{:S(2)}) %collective-permute-start.13) | collective-permute-done | bytes 245792 | tf_op jit(solution)/shard_map/ppermute | solution.py:50
  106.6 9.1 %collective-permute-done.6 = f32[5,2,48,128]{3,2,1,0:T(8,128)S(1)} collective-permute-done((f32[5,2,48,128]{3,2,1,0:T(8,128)S(1)}, f32[5,2,48,128]{3,2,1,0:T(8,128)S(1)}, u32[]{:S(2)}, u32[]{:S(2)}) %collective-permute-start.6) | collective-permute-done | bytes 245792 | tf_op jit(solution)/shard_map/ppermute | solution.py:50
  120.6 11.0 %collective-permute-start.7 = (f32[5,4,48,128]{3,2,1,0:T(8,128)S(1)}, f32[5,4,48,128]{3,2,1,0:T(8,128)S(1)}, u32[]{:S(2)}, u32[]{:S(2)}) collective-permute-start(f32[5,4,48,128]{3,2,1,0:T(8,128)S(1)} %constant_dynamic-slice_fusion.1), channel_id=1, source_target_pairs={{504,0},{0,8},{8,16},{16,24},{24,32},{32,40},{40,48},{48,56},{56,6... | collective-permute-start | bytes 1474568 | tf_op jit(solution)/shard_map/ppermute | solution.py:17
  131.9 5.5 %collective-permute-done.7 = f32[5,4,48,128]{3,2,1,0:T(8,128)S(1)} collective-permute-done((f32[5,4,48,128]{3,2,1,0:T(8,128)S(1)}, f32[5,4,48,128]{3,2,1,0:T(8,128)S(1)}, u32[]{:S(2)}, u32[]{:S(2)}) %collective-permute-start.7) | collective-permute-done | bytes 491552 | tf_op jit(solution)/shard_map/ppermute | solution.py:17
  139.4 7.1 %collective-permute-start.14 = (f32[3,4,48,128]{3,2,1,0:T(8,128)S(1)}, f32[3,4,48,128]{3,2,1,0:T(8,128)S(1)}, u32[]{:S(2)}, u32[]{:S(2)}) collective-permute-start(f32[3,4,48,128]{3,2,1,0:T(8,128)S(1)} %get-tuple-element.21), channel_id=1, source_target_pairs={{0,8},{8,16},{16,24},{24,32},{32,40},{40,48},{48,56},{56,64},{64,7... | collective-permute-start | bytes 884744 | tf_op jit(solution)/shard_map/ppermute | solution.py:27
  150.8 6.4 %collective-permute-done.15 = f32[3,4,48,128]{3,2,1,0:T(8,128)S(1)} collective-permute-done((f32[3,4,48,128]{3,2,1,0:T(8,128)S(1)}, f32[3,4,48,128]{3,2,1,0:T(8,128)S(1)}, u32[]{:S(2)}, u32[]{:S(2)}) %collective-permute-start.15) | collective-permute-done | bytes 294944 | tf_op jit(solution)/shard_map/ppermute | solution.py:30
  161.1 6.3 %collective-permute-start.19 = (f32[3,1,48,128]{3,2,1,0:T(8,128)S(1)}, f32[3,1,48,128]{3,2,1,0:T(8,128)S(1)}, u32[]{:S(2)}, u32[]{:S(2)}) collective-permute-start(f32[3,1,48,128]{3,2,1,0:T(8,128)S(1)} %get-tuple-element.20), channel_id=1, source_target_pairs={{0,8},{8,16},{16,24},{24,32},{32,40},{40,48},{48,56},{56,64},{64,7... | collective-permute-start | bytes 221192 | tf_op jit(solution)/shard_map/ppermute | solution.py:27
  169.4 3.4 %collective-permute-start.17 = (f32[3,16,1,128]{3,2,1,0:T(1,128)S(1)}, f32[3,16,1,128]{3,2,1,0:T(1,128)S(1)}, u32[]{:S(2)}, u32[]{:S(2)}) collective-permute-start(f32[3,16,1,128]{3,2,1,0:T(1,128)S(1)} %get-tuple-element.14), channel_id=1, source_target_pairs={{0,1},{1,2},{2,3},{3,4},{4,5},{5,6},{6,7},{8,9},{9,10},{10,11},{11... | collective-permute-start | bytes 73736 | tf_op jit(solution)/shard_map/ppermute | solution.py:27
  173.4 6.5 %collective-permute-done.17 = f32[3,16,1,128]{3,2,1,0:T(1,128)S(1)} collective-permute-done((f32[3,16,1,128]{3,2,1,0:T(1,128)S(1)}, f32[3,16,1,128]{3,2,1,0:T(1,128)S(1)}, u32[]{:S(2)}, u32[]{:S(2)}) %collective-permute-start.17) | collective-permute-done | bytes 24608 | tf_op jit(solution)/shard_map/ppermute | solution.py:27
  (80 shorter events, 36.0 us)
Async XLA Ops:
  1.7 1.5 copy-start.1
  3.2 2.7 %copy-start.4 = (s32[4]{0:T(128)S(1)}, s32[4]{0:T(128)}, u32[]{:S(2)}) copy-start(s32[4]{0:T(128)} %param.6) | copy-start | bytes 52
  3.2 13.4 %collective-permute-start = (f32[5,4,48,128]{3,2,1,0:T(8,128)S(1)}, f32[5,4,48,128]{3,2,1,0:T(8,128)S(1)}, u32[]{:S(2)}, u32[]{:S(2)}) collective-permute-start(f32[5,4,48,128]{3,2,1,0:T(8,128)S(1)} %pad_maximum_fusion.7), channel_id=1, source_target_pairs={{8,0},{16,8},{24,16},{32,24},{40,32},{48,40},{56,48},{64,56},{72,6... | collective-permute-start | bytes 1474568 | tf_op jit(solution)/shard_map/ppermute | solution.py:17
  17.2 12.5 %copy-start.3 = (s32[128]{0:T(128)S(1)}, s32[128]{0:T(128)}, u32[]{:S(2)}) copy-start(s32[128]{0:T(128)} %param.7) | copy-start | bytes 1540
  17.2 17.8 %collective-permute-start.8 = (f32[5,2,48,128]{3,2,1,0:T(8,128)S(1)}, f32[5,2,48,128]{3,2,1,0:T(8,128)S(1)}, u32[]{:S(2)}, u32[]{:S(2)}) collective-permute-start(f32[5,2,48,128]{3,2,1,0:T(8,128)S(1)} %fusion.54), channel_id=1, source_target_pairs={{0,128},{128,256},{256,384},{384,0},{1,129},{129,257},{257,385},{3... | collective-permute-start | bytes 737288 | tf_op jit(solution)/shard_map/ppermute | solution.py:47
  24.3 12.7 %collective-permute-start.1 = (f32[5,2,48,128]{3,2,1,0:T(8,128)S(1)}, f32[5,2,48,128]{3,2,1,0:T(8,128)S(1)}, u32[]{:S(2)}, u32[]{:S(2)}) collective-permute-start(f32[5,2,48,128]{3,2,1,0:T(8,128)S(1)} %fusion.61), channel_id=1, source_target_pairs={{0,384},{128,0},{256,128},{384,256},{1,385},{129,1},{257,129},{385... | collective-permute-start | bytes 737288 | tf_op jit(solution)/shard_map/ppermute | solution.py:47
  35.1 13.6 %collective-permute-start.9 = (f32[5,2,48,128]{3,2,1,0:T(8,128)S(1)}, f32[5,2,48,128]{3,2,1,0:T(8,128)S(1)}, u32[]{:S(2)}, u32[]{:S(2)}) collective-permute-start(f32[5,2,48,128]{3,2,1,0:T(8,128)S(1)} %fusion.56), channel_id=1, source_target_pairs={{0,128},{128,256},{256,384},{384,0},{1,129},{129,257},{257,385},{3... | collective-permute-start | bytes 737288 | tf_op jit(solution)/shard_map/ppermute | solution.py:47
  37.1 15.7 %collective-permute-start.2 = (f32[5,2,48,128]{3,2,1,0:T(8,128)S(1)}, f32[5,2,48,128]{3,2,1,0:T(8,128)S(1)}, u32[]{:S(2)}, u32[]{:S(2)}) collective-permute-start(f32[5,2,48,128]{3,2,1,0:T(8,128)S(1)} %fusion.63), channel_id=1, source_target_pairs={{0,384},{128,0},{256,128},{384,256},{1,385},{129,1},{257,129},{385... | collective-permute-start | bytes 737288 | tf_op jit(solution)/shard_map/ppermute | solution.py:47
  48.7 13.4 %collective-permute-start.10 = (f32[5,2,48,128]{3,2,1,0:T(8,128)S(1)}, f32[5,2,48,128]{3,2,1,0:T(8,128)S(1)}, u32[]{:S(2)}, u32[]{:S(2)}) collective-permute-start(f32[5,2,48,128]{3,2,1,0:T(8,128)S(1)} %fusion.58), channel_id=1, source_target_pairs={{0,128},{128,256},{256,384},{384,0},{1,129},{129,257},{257,385},{3... | collective-permute-start | bytes 737288 | tf_op jit(solution)/shard_map/ppermute | solution.py:47
  52.9 11.3 %collective-permute-start.3 = (f32[5,2,48,128]{3,2,1,0:T(8,128)S(1)}, f32[5,2,48,128]{3,2,1,0:T(8,128)S(1)}, u32[]{:S(2)}, u32[]{:S(2)}) collective-permute-start(f32[5,2,48,128]{3,2,1,0:T(8,128)S(1)} %fusion.65), channel_id=1, source_target_pairs={{0,384},{128,0},{256,128},{384,256},{1,385},{129,1},{257,129},{385... | collective-permute-start | bytes 737288 | tf_op jit(solution)/shard_map/ppermute | solution.py:47
  62.2 16.3 %collective-permute-start.11 = (f32[5,2,48,128]{3,2,1,0:T(8,128)S(1)}, f32[5,2,48,128]{3,2,1,0:T(8,128)S(1)}, u32[]{:S(2)}, u32[]{:S(2)}) collective-permute-start(f32[5,2,48,128]{3,2,1,0:T(8,128)S(1)} %fusion.53), channel_id=1, source_target_pairs={{0,128},{128,256},{256,384},{384,0},{1,129},{129,257},{257,385},{3... | collective-permute-start | bytes 737288 | tf_op jit(solution)/shard_map/ppermute | solution.py:50
  64.9 16.1 %collective-permute-start.4 = (f32[5,2,48,128]{3,2,1,0:T(8,128)S(1)}, f32[5,2,48,128]{3,2,1,0:T(8,128)S(1)}, u32[]{:S(2)}, u32[]{:S(2)}) collective-permute-start(f32[5,2,48,128]{3,2,1,0:T(8,128)S(1)} %get-tuple-element.5), channel_id=1, source_target_pairs={{0,384},{128,0},{256,128},{384,256},{1,385},{129,1},{257,129},{385... | collective-permute-start | bytes 737288 | tf_op jit(solution)/shard_map/ppermute | solution.py:50
  78.5 15.5 %collective-permute-start.12 = (f32[5,2,48,128]{3,2,1,0:T(8,128)S(1)}, f32[5,2,48,128]{3,2,1,0:T(8,128)S(1)}, u32[]{:S(2)}, u32[]{:S(2)}) collective-permute-start(f32[5,2,48,128]{3,2,1,0:T(8,128)S(1)} %collective-permute-done.11), channel_id=1, source_target_pairs={{0,128},{128,256},{256,384},{384,0},{1,129},{129,257},{257,385},{3... | collective-permute-start | bytes 737288 | tf_op jit(solution)/shard_map/ppermute | solution.py:50
  81.0 17.0 %collective-permute-start.5 = (f32[5,2,48,128]{3,2,1,0:T(8,128)S(1)}, f32[5,2,48,128]{3,2,1,0:T(8,128)S(1)}, u32[]{:S(2)}, u32[]{:S(2)}) collective-permute-start(f32[5,2,48,128]{3,2,1,0:T(8,128)S(1)} %collective-permute-done.4), channel_id=1, source_target_pairs={{0,384},{128,0},{256,128},{384,256},{1,385},{129,1},{257,129},{385... | collective-permute-start | bytes 737288 | tf_op jit(solution)/shard_map/ppermute | solution.py:50
  94.0 12.5 %collective-permute-start.13 = (f32[5,2,48,128]{3,2,1,0:T(8,128)S(1)}, f32[5,2,48,128]{3,2,1,0:T(8,128)S(1)}, u32[]{:S(2)}, u32[]{:S(2)}) collective-permute-start(f32[5,2,48,128]{3,2,1,0:T(8,128)S(1)} %collective-permute-done.12), channel_id=1, source_target_pairs={{0,128},{128,256},{256,384},{384,0},{1,129},{129,257},{257,385},{3... | collective-permute-start | bytes 737288 | tf_op jit(solution)/shard_map/ppermute | solution.py:50
  98.0 17.8 %collective-permute-start.6 = (f32[5,2,48,128]{3,2,1,0:T(8,128)S(1)}, f32[5,2,48,128]{3,2,1,0:T(8,128)S(1)}, u32[]{:S(2)}, u32[]{:S(2)}) collective-permute-start(f32[5,2,48,128]{3,2,1,0:T(8,128)S(1)} %collective-permute-done.5), channel_id=1, source_target_pairs={{0,384},{128,0},{256,128},{384,256},{1,385},{129,1},{257,129},{385... | collective-permute-start | bytes 737288 | tf_op jit(solution)/shard_map/ppermute | solution.py:50
  119.3 12.3 %copy-start.2 = (f32[5,16,48,128]{3,2,1,0:T(8,128)S(1)}, f32[5,16,48,128]{3,2,1,0:T(8,128)}, u32[]{:S(2)}) copy-start(f32[5,16,48,128]{3,2,1,0:T(8,128)} %constant_dynamic-update-slice_fusion) | copy-start | bytes 5898244
  120.6 16.8 %collective-permute-start.7 = (f32[5,4,48,128]{3,2,1,0:T(8,128)S(1)}, f32[5,4,48,128]{3,2,1,0:T(8,128)S(1)}, u32[]{:S(2)}, u32[]{:S(2)}) collective-permute-start(f32[5,4,48,128]{3,2,1,0:T(8,128)S(1)} %constant_dynamic-slice_fusion.1), channel_id=1, source_target_pairs={{504,0},{0,8},{8,16},{16,24},{24,32},{32,40},{40,48},{48,56},{56,6... | collective-permute-start | bytes 1474568 | tf_op jit(solution)/shard_map/ppermute | solution.py:17
  139.4 11.4 %collective-permute-start.14 = (f32[3,4,48,128]{3,2,1,0:T(8,128)S(1)}, f32[3,4,48,128]{3,2,1,0:T(8,128)S(1)}, u32[]{:S(2)}, u32[]{:S(2)}) collective-permute-start(f32[3,4,48,128]{3,2,1,0:T(8,128)S(1)} %get-tuple-element.21), channel_id=1, source_target_pairs={{0,8},{8,16},{16,24},{24,32},{32,40},{40,48},{48,56},{56,64},{64,7... | collective-permute-start | bytes 884744 | tf_op jit(solution)/shard_map/ppermute | solution.py:27
  146.5 10.7 %collective-permute-start.15 = (f32[3,4,48,128]{3,2,1,0:T(8,128)S(1)}, f32[3,4,48,128]{3,2,1,0:T(8,128)S(1)}, u32[]{:S(2)}, u32[]{:S(2)}) collective-permute-start(f32[3,4,48,128]{3,2,1,0:T(8,128)S(1)} %get-tuple-element.22), channel_id=1, source_target_pairs={{8,0},{16,8},{24,16},{32,24},{40,32},{48,40},{56,48},{64,56},{72,6... | collective-permute-start | bytes 884744 | tf_op jit(solution)/shard_map/ppermute | solution.py:30
  159.2 20.8 %collective-permute-start.18 = (f32[3,1,48,128]{3,2,1,0:T(8,128)S(1)}, f32[3,1,48,128]{3,2,1,0:T(8,128)S(1)}, u32[]{:S(2)}, u32[]{:S(2)}) collective-permute-start(f32[3,1,48,128]{3,2,1,0:T(8,128)S(1)} %get-tuple-element.19), channel_id=1, source_target_pairs={{8,0},{16,8},{24,16},{32,24},{40,32},{48,40},{56,48},{64,56},{72,6... | collective-permute-start | bytes 221192 | tf_op jit(solution)/shard_map/ppermute | solution.py:30
  161.1 18.9 %collective-permute-start.19 = (f32[3,1,48,128]{3,2,1,0:T(8,128)S(1)}, f32[3,1,48,128]{3,2,1,0:T(8,128)S(1)}, u32[]{:S(2)}, u32[]{:S(2)}) collective-permute-start(f32[3,1,48,128]{3,2,1,0:T(8,128)S(1)} %get-tuple-element.20), channel_id=1, source_target_pairs={{0,8},{8,16},{16,24},{24,32},{32,40},{40,48},{48,56},{56,64},{64,7... | collective-permute-start | bytes 221192 | tf_op jit(solution)/shard_map/ppermute | solution.py:27
  167.5 6.0 %collective-permute-start.16 = (f32[3,16,1,128]{3,2,1,0:T(1,128)S(1)}, f32[3,16,1,128]{3,2,1,0:T(1,128)S(1)}, u32[]{:S(2)}, u32[]{:S(2)}) collective-permute-start(f32[3,16,1,128]{3,2,1,0:T(1,128)S(1)} %get-tuple-element.13), channel_id=1, source_target_pairs={{1,0},{2,1},{3,2},{4,3},{5,4},{6,5},{7,6},{9,8},{10,9},{11,10},{12... | collective-permute-start | bytes 73736 | tf_op jit(solution)/shard_map/ppermute | solution.py:30
  169.4 10.6 %collective-permute-start.17 = (f32[3,16,1,128]{3,2,1,0:T(1,128)S(1)}, f32[3,16,1,128]{3,2,1,0:T(1,128)S(1)}, u32[]{:S(2)}, u32[]{:S(2)}) collective-permute-start(f32[3,16,1,128]{3,2,1,0:T(1,128)S(1)} %get-tuple-element.14), channel_id=1, source_target_pairs={{0,1},{1,2},{2,3},{3,4},{4,5},{5,6},{6,7},{8,9},{9,10},{10,11},{11... | collective-permute-start | bytes 73736 | tf_op jit(solution)/shard_map/ppermute | solution.py:27
  (1 other events, 1.4 us)

commit v3 on v2

--- a/solution.py
+++ b/solution.py
@@ -118,35 +118,58 @@
     return -0.5 * (diagonal_part + 2.0 * cross_part)
 
 
+def carry(raw):
+    return jnp.concatenate([raw[0:1], raw[0:1] * raw[1:4], raw[4:5]], axis=0)
+
+
 def shards(density, flow_vars, blade_offset, smooth_width):
     cells = density.shape[0]
     rad_cells = density.shape[1]
     group = lax.axis_size("slab")
     blade = lax.axis_index("blade")
-    own_offset = jnp.sum(jnp.where(jnp.arange(BLADES) == blade, blade_offset, 0))
+    slab = lax.axis_index("slab")
+
+    def offset_of(which):
+        return jnp.sum(jnp.where(jnp.arange(BLADES) == which, blade_offset, 0))
+
+    own_offset = offset_of(blade)
+    prev_offset = offset_of(jnp.where(slab == 0, (blade + BLADES - 1) % BLADES, blade))
+    next_offset = offset_of(jnp.where(slab == group - 1, (blade + 1) % BLADES, blade))
+    reach = HW + 1
     velocity = flow_vars[0:3]
-    carried = jnp.concatenate([density[None], density[None] * velocity, flow_vars[3:4]], axis=0)
-    ahead = passed_along(carried[:, :MAXOFF], AZ, -1)
+    raw = jnp.concatenate([density[None], flow_vars], axis=0)
+    from_next = passed_along(raw[:, :reach], AZ, -1)
+    from_prev = passed_along(velocity[:, cells - reach :], AZ, 1)
+    carried = carry(raw)
+    ahead = carry(from_next[:, :MAXOFF])
     contribution = lax.dynamic_slice_in_dim(
         jnp.concatenate([carried, ahead], axis=1), own_offset, cells, 1
     )
     sector_part = ring_sum(contribution)
-    behind = passed_along(sector_part[:, cells - MAXOFF :], AZ, 1)
-    phase_sums = lax.dynamic_slice_in_dim(
-        jnp.concatenate([behind, sector_part], axis=1), MAXOFF - own_offset, cells, 1
+    margin = MAXOFF + reach
+    prev_part = passed_along(sector_part[:, cells - margin :], AZ, 1)
+    next_part = passed_along(sector_part[:, :reach], AZ, -1)
+    window = jnp.concatenate([prev_part, sector_part, next_part], axis=1)
+    sums = jnp.concatenate(
+        [
+            lax.dynamic_slice_in_dim(window, MAXOFF - prev_offset, reach, 1),
+            lax.dynamic_slice_in_dim(window, margin - own_offset, cells, 1),
+            lax.dynamic_slice_in_dim(window, cells + margin - next_offset, reach, 1),
+        ],
+        axis=1,
     )
-    mean_fields = jnp.concatenate(
-        [phase_sums[0:1] / BLADES, phase_sums[1:4] / phase_sums[0:1], phase_sums[4:5] / BLADES],
-        axis=0,
+    means = jnp.concatenate(
+        [sums[0:1] / BLADES, sums[1:4] / sums[0:1], sums[4:5] / BLADES], axis=0
     )
-    fluctuation = velocity - mean_fields[1:4]
+    mean_fields = means[:, reach : reach + cells]
+    moving = jnp.concatenate([from_prev, velocity, from_next[1:4]], axis=1)
+    fluctuation = moving - means[1:4]
     taps = smoothing_taps(smooth_width)
-    rimmed = extended(fluctuation, ((AZ, 1),), HW, True)
-    smoothed = apply_taps(rimmed, taps, cells)
-    az_side = extended(smoothed, ((AZ, 1),), 1, True)
+    rimmed = apply_taps(fluctuation, taps, cells + 2)
+    smoothed = rimmed[:, 1 : cells + 1]
     rad_side = extended(smoothed, (("rad", 2),), 1, False)
     dtheta = 2.0 * math.pi / (cells * lax.axis_size(AZ))
-    az_rate = (az_side[:, 2:] - az_side[:, :-2]) / (2.0 * dtheta)
+    az_rate = (rimmed[:, 2:] - rimmed[:, :-2]) / (2.0 * dtheta)
     total_rad = rad_cells * lax.axis_size("rad")
     rows = lax.axis_index("rad") * rad_cells + jnp.arange(rad_cells)
     upper = jnp.where((rows == total_rad - 1)[:, None], smoothed, rad_side[:, :, 2:])

time: 182 us -> 186 us (1.022)
  the two profiles are of different devices: /device:TPU:121 before, /device:TPU:6 now
where the time goes in v3:
time: 186 us; the launch traced here: 185 us
  starting transfers between devices  96.6 us (52%)
  waiting for transfers between devices  52 us (28%)
  other arithmetic  22.6 us (12%)
  between operations  6.88 us (4%)
  local copies, waits for them, and re-layouts  6.61 us (4%)
    ppermute x6, starting transfers between devices, ring_half(): pieces.append(lax.ppermute(pieces[-1], 'blade', route))  30.8 us
    ppermute x4, starting transfers between devices, passed_along(): return lax.ppermute(block, axis, route)  24.8 us
    ppermute x6, starting transfers between devices, ring_half(): lax.ppermute(total, 'blade', route) + piece((place - step * turn) % count)  24.1 us
    ppermute x6, waiting for transfers between devices, ring_half(): pieces.append(lax.ppermute(pieces[-1], 'blade', route))  20.8 us
    ppermute x1, starting transfers between devices, extended(): lax.ppermute(lax.slice_in_dim(block, block.shape[dim] - width, None, axis...  15 us
    ppermute x6, waiting for transfers between devices, ring_half(): lax.ppermute(total, 'blade', route) + piece((place - step * turn) % count)  13.1 us
    ppermute x4, waiting for transfers between devices, passed_along(): return lax.ppermute(block, axis, route)  10.5 us
    add x5, other arithmetic, ring_half(): lax.ppermute(total, 'blade', route) + piece((place - step * turn) % count)  7.73 us
  transfers between devices with their start and end apart: 18, of which 11 were waited for; matrix products, arithmetic and copies ran while one was open for 11% of the time, Pallas kernels for 0%

profile of v3, /device:TPU:6, one launch (start us, length us, event | category | flops | bytes accessed | tf_op | source)
XLA Modules:
  0.0 184.7 jit_solution(7805304772399151771)
XLA Ops:
  1.9 13.4 %collective-permute-start = (f32[5,5,48,128]{3,2,1,0:T(8,128)S(1)}, f32[5,5,48,128]{3,2,1,0:T(8,128)S(1)}, u32[]{:S(2)}, u32[]{:S(2)}) collective-permute-start(f32[5,5,48,128]{3,2,1,0:T(8,128)S(1)} %pad_maximum_fusion.8), channel_id=1, source_target_pairs={{8,0},{16,8},{24,16},{32,24},{40,32},{48,40},{56,48},{64,56},{72,6... | collective-permute-start | bytes 1843208 | tf_op jit(solution)/shard_map/ppermute | solution.py:17
  19.1 3.8 %collective-permute-done = f32[5,5,48,128]{3,2,1,0:T(8,128)S(1)} collective-permute-done((f32[5,5,48,128]{3,2,1,0:T(8,128)S(1)}, f32[5,5,48,128]{3,2,1,0:T(8,128)S(1)}, u32[]{:S(2)}, u32[]{:S(2)}) %collective-permute-start) | collective-permute-done | bytes 614432 | tf_op jit(solution)/shard_map/ppermute | solution.py:17
  27.9 6.0 %collective-permute-start.7 = (f32[5,2,48,128]{3,2,1,0:T(8,128)}, f32[5,2,48,128]{3,2,1,0:T(8,128)}, u32[]{:S(2)}, u32[]{:S(2)}) collective-permute-start(f32[5,2,48,128]{3,2,1,0:T(8,128)} %fusion.39), channel_id=1, source_target_pairs={{0,384},{128,0},{256,128},{384,256},{1,385},{129,1},{257,129},{385... | collective-permute-start | bytes 737288 | tf_op jit(solution)/shard_map/ppermute | solution.py:47
  34.0 4.8 %collective-permute-done.1 = f32[5,2,48,128]{3,2,1,0:T(8,128)} collective-permute-done((f32[5,2,48,128]{3,2,1,0:T(8,128)}, f32[5,2,48,128]{3,2,1,0:T(8,128)}, u32[]{:S(2)}, u32[]{:S(2)}) %collective-permute-start.1) | collective-permute-done | bytes 245792 | tf_op jit(solution)/shard_map/ppermute | solution.py:47
  40.4 2.9 %collective-permute-start.2 = (f32[5,2,48,128]{3,2,1,0:T(8,128)}, f32[5,2,48,128]{3,2,1,0:T(8,128)}, u32[]{:S(2)}, u32[]{:S(2)}) collective-permute-start(f32[5,2,48,128]{3,2,1,0:T(8,128)} %fusion.48), channel_id=1, source_target_pairs={{0,128},{128,256},{256,384},{384,0},{1,129},{129,257},{257,385},{3... | collective-permute-start | bytes 737288 | tf_op jit(solution)/shard_map/ppermute | solution.py:47
  45.0 5.1 %collective-permute-start.8 = (f32[5,2,48,128]{3,2,1,0:T(8,128)}, f32[5,2,48,128]{3,2,1,0:T(8,128)}, u32[]{:S(2)}, u32[]{:S(2)}) collective-permute-start(f32[5,2,48,128]{3,2,1,0:T(8,128)} %fusion.41), channel_id=1, source_target_pairs={{0,384},{128,0},{256,128},{384,256},{1,385},{129,1},{257,129},{385... | collective-permute-start | bytes 737288 | tf_op jit(solution)/shard_map/ppermute | solution.py:47
  50.1 3.0 %collective-permute-done.2 = f32[5,2,48,128]{3,2,1,0:T(8,128)} collective-permute-done((f32[5,2,48,128]{3,2,1,0:T(8,128)}, f32[5,2,48,128]{3,2,1,0:T(8,128)}, u32[]{:S(2)}, u32[]{:S(2)}) %collective-permute-start.2) | collective-permute-done | bytes 245792 | tf_op jit(solution)/shard_map/ppermute | solution.py:47
  54.8 4.8 %collective-permute-start.3 = (f32[5,2,48,128]{3,2,1,0:T(8,128)}, f32[5,2,48,128]{3,2,1,0:T(8,128)}, u32[]{:S(2)}, u32[]{:S(2)}) collective-permute-start(f32[5,2,48,128]{3,2,1,0:T(8,128)} %fusion.50), channel_id=1, source_target_pairs={{0,128},{128,256},{256,384},{384,0},{1,129},{129,257},{257,385},{3... | collective-permute-start | bytes 737288 | tf_op jit(solution)/shard_map/ppermute | solution.py:47
  61.4 3.4 %collective-permute-start.9 = (f32[5,2,48,128]{3,2,1,0:T(8,128)}, f32[5,2,48,128]{3,2,1,0:T(8,128)}, u32[]{:S(2)}, u32[]{:S(2)}) collective-permute-start(f32[5,2,48,128]{3,2,1,0:T(8,128)} %fusion.43), channel_id=1, source_target_pairs={{0,384},{128,0},{256,128},{384,256},{1,385},{129,1},{257,129},{385... | collective-permute-start | bytes 737288 | tf_op jit(solution)/shard_map/ppermute | solution.py:47
  64.8 5.0 %collective-permute-done.3 = f32[5,2,48,128]{3,2,1,0:T(8,128)} collective-permute-done((f32[5,2,48,128]{3,2,1,0:T(8,128)}, f32[5,2,48,128]{3,2,1,0:T(8,128)}, u32[]{:S(2)}, u32[]{:S(2)}) %collective-permute-start.3) | collective-permute-done | bytes 245792 | tf_op jit(solution)/shard_map/ppermute | solution.py:47
  70.9 6.1 %collective-permute-start.4 = (f32[5,2,48,128]{3,2,1,0:T(8,128)S(1)}, f32[5,2,48,128]{3,2,1,0:T(8,128)S(1)}, u32[]{:S(2)}, u32[]{:S(2)}) collective-permute-start(f32[5,2,48,128]{3,2,1,0:T(8,128)S(1)} %fusion.45), channel_id=1, source_target_pairs={{0,128},{128,256},{256,384},{384,0},{1,129},{129,257},{257,385},{3... | collective-permute-start | bytes 737288 | tf_op jit(solution)/shard_map/ppermute | solution.py:50
  78.9 3.0 %collective-permute-start.10 = (f32[5,2,48,128]{3,2,1,0:T(8,128)S(1)}, f32[5,2,48,128]{3,2,1,0:T(8,128)S(1)}, u32[]{:S(2)}, u32[]{:S(2)}) collective-permute-start(f32[5,2,48,128]{3,2,1,0:T(8,128)S(1)} %get-tuple-element.10), channel_id=1, source_target_pairs={{0,384},{128,0},{256,128},{384,256},{1,385},{129,1},{257,129},{385... | collective-permute-start | bytes 737288 | tf_op jit(solution)/shard_map/ppermute | solution.py:50
  81.9 4.4 %collective-permute-done.4 = f32[5,2,48,128]{3,2,1,0:T(8,128)S(1)} collective-permute-done((f32[5,2,48,128]{3,2,1,0:T(8,128)S(1)}, f32[5,2,48,128]{3,2,1,0:T(8,128)S(1)}, u32[]{:S(2)}, u32[]{:S(2)}) %collective-permute-start.4) | collective-permute-done | bytes 245792 | tf_op jit(solution)/shard_map/ppermute | solution.py:50
  86.3 4.8 %collective-permute-start.5 = (f32[5,2,48,128]{3,2,1,0:T(8,128)S(1)}, f32[5,2,48,128]{3,2,1,0:T(8,128)S(1)}, u32[]{:S(2)}, u32[]{:S(2)}) collective-permute-start(f32[5,2,48,128]{3,2,1,0:T(8,128)S(1)} %collective-permute-done.4), channel_id=1, source_target_pairs={{0,128},{128,256},{256,384},{384,0},{1,129},{129,257},{257,385},{3... | collective-permute-start | bytes 737288 | tf_op jit(solution)/shard_map/ppermute | solution.py:50
  93.8 3.4 %collective-permute-start.11 = (f32[5,2,48,128]{3,2,1,0:T(8,128)S(1)}, f32[5,2,48,128]{3,2,1,0:T(8,128)S(1)}, u32[]{:S(2)}, u32[]{:S(2)}) collective-permute-start(f32[5,2,48,128]{3,2,1,0:T(8,128)S(1)} %collective-permute-done.10), channel_id=1, source_target_pairs={{0,384},{128,0},{256,128},{384,256},{1,385},{129,1},{257,129},{385... | collective-permute-start | bytes 737288 | tf_op jit(solution)/shard_map/ppermute | solution.py:50
  97.3 4.3 %collective-permute-done.5 = f32[5,2,48,128]{3,2,1,0:T(8,128)S(1)} collective-permute-done((f32[5,2,48,128]{3,2,1,0:T(8,128)S(1)}, f32[5,2,48,128]{3,2,1,0:T(8,128)S(1)}, u32[]{:S(2)}, u32[]{:S(2)}) %collective-permute-start.5) | collective-permute-done | bytes 245792 | tf_op jit(solution)/shard_map/ppermute | solution.py:50
  101.6 11.6 %collective-permute-start.6 = (f32[5,2,48,128]{3,2,1,0:T(8,128)S(1)}, f32[5,2,48,128]{3,2,1,0:T(8,128)S(1)}, u32[]{:S(2)}, u32[]{:S(2)}) collective-permute-start(f32[5,2,48,128]{3,2,1,0:T(8,128)S(1)} %collective-permute-done.5), channel_id=1, source_target_pairs={{0,128},{128,256},{256,384},{384,0},{1,129},{129,257},{257,385},{3... | collective-permute-start | bytes 737288 | tf_op jit(solution)/shard_map/ppermute | solution.py:50
  116.6 3.9 %collective-permute-done.6 = f32[5,2,48,128]{3,2,1,0:T(8,128)S(1)} collective-permute-done((f32[5,2,48,128]{3,2,1,0:T(8,128)S(1)}, f32[5,2,48,128]{3,2,1,0:T(8,128)S(1)}, u32[]{:S(2)}, u32[]{:S(2)}) %collective-permute-start.6) | collective-permute-done | bytes 245792 | tf_op jit(solution)/shard_map/ppermute | solution.py:50
  120.7 8.2 %collective-permute-done.12 = f32[5,2,48,128]{3,2,1,0:T(8,128)S(1)} collective-permute-done((f32[5,2,48,128]{3,2,1,0:T(8,128)S(1)}, f32[5,2,48,128]{3,2,1,0:T(8,128)S(1)}, u32[]{:S(2)}, u32[]{:S(2)}) %collective-permute-start.12) | collective-permute-done | bytes 245792 | tf_op jit(solution)/shard_map/ppermute | solution.py:50
  133.1 7.5 %collective-permute-start.14 = (f32[5,5,48,128]{3,2,1,0:T(8,128)}, f32[5,5,48,128]{3,2,1,0:T(8,128)}, u32[]{:S(2)}, u32[]{:S(2)}) collective-permute-start(f32[5,5,48,128]{3,2,1,0:T(8,128)} %constant_dynamic-slice_fusion.5), channel_id=1, source_target_pairs={{8,0},{16,8},{24,16},{32,24},{40,32},{48,40},{56,48},{64,56},{72,6... | collective-permute-start | bytes 1843208 | tf_op jit(solution)/shard_map/ppermute | solution.py:17
  144.6 6.7 %collective-permute-done.14 = f32[5,5,48,128]{3,2,1,0:T(8,128)} collective-permute-done((f32[5,5,48,128]{3,2,1,0:T(8,128)}, f32[5,5,48,128]{3,2,1,0:T(8,128)}, u32[]{:S(2)}, u32[]{:S(2)}) %collective-permute-start.14) | collective-permute-done | bytes 614432 | tf_op jit(solution)/shard_map/ppermute | solution.py:17
  156.5 15.0 %collective-permute-start.17 = (f32[3,16,1,128]{3,2,1,0:T(1,128)S(1)}, f32[3,16,1,128]{3,2,1,0:T(1,128)S(1)}, u32[]{:S(2)}, u32[]{:S(2)}) collective-permute-start(f32[3,16,1,128]{3,2,1,0:T(1,128)S(1)} %get-tuple-element.19), channel_id=1, source_target_pairs={{0,1},{1,2},{2,3},{3,4},{4,5},{5,6},{6,7},{8,9},{9,10},{10,11},{11... | collective-permute-start | bytes 73736 | tf_op jit(solution)/shard_map/ppermute | solution.py:27
  171.4 1.9 %collective-permute-start.16 = (f32[3,16,1,128]{3,2,1,0:T(1,128)S(1)}, f32[3,16,1,128]{3,2,1,0:T(1,128)S(1)}, u32[]{:S(2)}, u32[]{:S(2)}) collective-permute-start(f32[3,16,1,128]{3,2,1,0:T(1,128)S(1)} %get-tuple-element.18), channel_id=1, source_target_pairs={{1,0},{2,1},{3,2},{4,3},{5,4},{6,5},{7,6},{9,8},{10,9},{11,10},{12... | collective-permute-start | bytes 73736 | tf_op jit(solution)/shard_map/ppermute | solution.py:30
  175.6 7.6 %collective-permute-done.16 = f32[3,16,1,128]{3,2,1,0:T(1,128)S(1)} collective-permute-done((f32[3,16,1,128]{3,2,1,0:T(1,128)S(1)}, f32[3,16,1,128]{3,2,1,0:T(1,128)S(1)}, u32[]{:S(2)}, u32[]{:S(2)}) %collective-permute-start.16) | collective-permute-done | bytes 24608 | tf_op jit(solution)/shard_map/ppermute | solution.py:30
  (92 shorter events, 37.1 us)
Async XLA Ops:
  0.6 17.2 %copy-start.2 = (f32[16,48,128]{2,1,0:T(8,128)S(1)}, f32[16,48,128]{2,1,0:T(8,128)}, u32[]{:S(2)}) copy-start(f32[16,48,128]{2,1,0:T(8,128)} %param.4) | copy-start | bytes 1179652
  0.6 17.2 %copy-start = (f32[4,16,48,128]{3,2,1,0:T(8,128)S(1)}, f32[4,16,48,128]{3,2,1,0:T(8,128)}, u32[]{:S(2)}) copy-start(f32[4,16,48,128]{3,2,1,0:T(8,128)} %param.5) | copy-start | bytes 4718596
  0.7 14.7 %copy-start.8 = (s32[4]{0:T(128)S(1)}, s32[4]{0:T(128)}, u32[]{:S(2)}) copy-start(s32[4]{0:T(128)} %param.6) | copy-start | bytes 52
  1.9 21.1 %collective-permute-start = (f32[5,5,48,128]{3,2,1,0:T(8,128)S(1)}, f32[5,5,48,128]{3,2,1,0:T(8,128)S(1)}, u32[]{:S(2)}, u32[]{:S(2)}) collective-permute-start(f32[5,5,48,128]{3,2,1,0:T(8,128)S(1)} %pad_maximum_fusion.8), channel_id=1, source_target_pairs={{8,0},{16,8},{24,16},{32,24},{40,32},{48,40},{56,48},{64,56},{72,6... | collective-permute-start | bytes 1843208 | tf_op jit(solution)/shard_map/ppermute | solution.py:17
  25.2 13.5 %collective-permute-start.1 = (f32[5,2,48,128]{3,2,1,0:T(8,128)}, f32[5,2,48,128]{3,2,1,0:T(8,128)}, u32[]{:S(2)}, u32[]{:S(2)}) collective-permute-start(f32[5,2,48,128]{3,2,1,0:T(8,128)} %fusion.46), channel_id=1, source_target_pairs={{0,128},{128,256},{256,384},{384,0},{1,129},{129,257},{257,385},{3... | collective-permute-start | bytes 737288 | tf_op jit(solution)/shard_map/ppermute | solution.py:47
  27.9 15.4 %collective-permute-start.7 = (f32[5,2,48,128]{3,2,1,0:T(8,128)}, f32[5,2,48,128]{3,2,1,0:T(8,128)}, u32[]{:S(2)}, u32[]{:S(2)}) collective-permute-start(f32[5,2,48,128]{3,2,1,0:T(8,128)} %fusion.39), channel_id=1, source_target_pairs={{0,384},{128,0},{256,128},{384,256},{1,385},{129,1},{257,129},{385... | collective-permute-start | bytes 737288 | tf_op jit(solution)/shard_map/ppermute | solution.py:47
  40.4 12.7 %collective-permute-start.2 = (f32[5,2,48,128]{3,2,1,0:T(8,128)}, f32[5,2,48,128]{3,2,1,0:T(8,128)}, u32[]{:S(2)}, u32[]{:S(2)}) collective-permute-start(f32[5,2,48,128]{3,2,1,0:T(8,128)} %fusion.48), channel_id=1, source_target_pairs={{0,128},{128,256},{256,384},{384,0},{1,129},{129,257},{257,385},{3... | collective-permute-start | bytes 737288 | tf_op jit(solution)/shard_map/ppermute | solution.py:47
  45.0 14.7 %collective-permute-start.8 = (f32[5,2,48,128]{3,2,1,0:T(8,128)}, f32[5,2,48,128]{3,2,1,0:T(8,128)}, u32[]{:S(2)}, u32[]{:S(2)}) collective-permute-start(f32[5,2,48,128]{3,2,1,0:T(8,128)} %fusion.41), channel_id=1, source_target_pairs={{0,384},{128,0},{256,128},{384,256},{1,385},{129,1},{257,129},{385... | collective-permute-start | bytes 737288 | tf_op jit(solution)/shard_map/ppermute | solution.py:47
  54.8 15.0 %collective-permute-start.3 = (f32[5,2,48,128]{3,2,1,0:T(8,128)}, f32[5,2,48,128]{3,2,1,0:T(8,128)}, u32[]{:S(2)}, u32[]{:S(2)}) collective-permute-start(f32[5,2,48,128]{3,2,1,0:T(8,128)} %fusion.50), channel_id=1, source_target_pairs={{0,128},{128,256},{256,384},{384,0},{1,129},{129,257},{257,385},{3... | collective-permute-start | bytes 737288 | tf_op jit(solution)/shard_map/ppermute | solution.py:47
  61.4 15.9 %collective-permute-start.9 = (f32[5,2,48,128]{3,2,1,0:T(8,128)}, f32[5,2,48,128]{3,2,1,0:T(8,128)}, u32[]{:S(2)}, u32[]{:S(2)}) collective-permute-start(f32[5,2,48,128]{3,2,1,0:T(8,128)} %fusion.43), channel_id=1, source_target_pairs={{0,384},{128,0},{256,128},{384,256},{1,385},{129,1},{257,129},{385... | collective-permute-start | bytes 737288 | tf_op jit(solution)/shard_map/ppermute | solution.py:47
  70.9 21.0 %copy-start.3 = (f32[5,2,48,128]{3,2,1,0:T(8,128)}, f32[5,2,48,128]{3,2,1,0:T(8,128)S(1)}, u32[]{:S(2)}) copy-start(f32[5,2,48,128]{3,2,1,0:T(8,128)S(1)} %fusion.45) | copy-start | bytes 737284
  70.9 15.4 %collective-permute-start.4 = (f32[5,2,48,128]{3,2,1,0:T(8,128)S(1)}, f32[5,2,48,128]{3,2,1,0:T(8,128)S(1)}, u32[]{:S(2)}, u32[]{:S(2)}) collective-permute-start(f32[5,2,48,128]{3,2,1,0:T(8,128)S(1)} %fusion.45), channel_id=1, source_target_pairs={{0,128},{128,256},{256,384},{384,0},{1,129},{129,257},{257,385},{3... | collective-permute-start | bytes 737288 | tf_op jit(solution)/shard_map/ppermute | solution.py:50
  78.9 14.9 %collective-permute-start.10 = (f32[5,2,48,128]{3,2,1,0:T(8,128)S(1)}, f32[5,2,48,128]{3,2,1,0:T(8,128)S(1)}, u32[]{:S(2)}, u32[]{:S(2)}) collective-permute-start(f32[5,2,48,128]{3,2,1,0:T(8,128)S(1)} %get-tuple-element.10), channel_id=1, source_target_pairs={{0,384},{128,0},{256,128},{384,256},{1,385},{129,1},{257,129},{385... | collective-permute-start | bytes 737288 | tf_op jit(solution)/shard_map/ppermute | solution.py:50
  86.3 15.3 %collective-permute-start.5 = (f32[5,2,48,128]{3,2,1,0:T(8,128)S(1)}, f32[5,2,48,128]{3,2,1,0:T(8,128)S(1)}, u32[]{:S(2)}, u32[]{:S(2)}) collective-permute-start(f32[5,2,48,128]{3,2,1,0:T(8,128)S(1)} %collective-permute-done.4), channel_id=1, source_target_pairs={{0,128},{128,256},{256,384},{384,0},{1,129},{129,257},{257,385},{3... | collective-permute-start | bytes 737288 | tf_op jit(solution)/shard_map/ppermute | solution.py:50
  91.9 61.6 %collective-permute-start.15 = (f32[3,5,48,128]{3,2,1,0:T(8,128)}, f32[3,5,48,128]{3,2,1,0:T(8,128)S(1)}, u32[]{:S(2)}, u32[]{:S(2)}) collective-permute-start(f32[3,5,48,128]{3,2,1,0:T(8,128)} %slice.201), channel_id=1, source_target_pairs={{504,0},{0,8},{8,16},{16,24},{24,32},{32,40},{40,48},{48,56},{56,6... | collective-permute-start | bytes 1105928 | tf_op jit(solution)/shard_map/ppermute | solution.py:17
  93.8 26.8 %copy-start.4 = (f32[5,2,48,128]{3,2,1,0:T(8,128)S(1)}, f32[5,2,48,128]{3,2,1,0:T(8,128)}, u32[]{:S(2)}) copy-start(f32[5,2,48,128]{3,2,1,0:T(8,128)} %copy-done.3) | copy-start | bytes 737284
  93.8 20.1 %collective-permute-start.11 = (f32[5,2,48,128]{3,2,1,0:T(8,128)S(1)}, f32[5,2,48,128]{3,2,1,0:T(8,128)S(1)}, u32[]{:S(2)}, u32[]{:S(2)}) collective-permute-start(f32[5,2,48,128]{3,2,1,0:T(8,128)S(1)} %collective-permute-done.10), channel_id=1, source_target_pairs={{0,384},{128,0},{256,128},{384,256},{1,385},{129,1},{257,129},{385... | collective-permute-start | bytes 737288 | tf_op jit(solution)/shard_map/ppermute | solution.py:50
  101.6 18.9 %collective-permute-start.6 = (f32[5,2,48,128]{3,2,1,0:T(8,128)S(1)}, f32[5,2,48,128]{3,2,1,0:T(8,128)S(1)}, u32[]{:S(2)}, u32[]{:S(2)}) collective-permute-start(f32[5,2,48,128]{3,2,1,0:T(8,128)S(1)} %collective-permute-done.5), channel_id=1, source_target_pairs={{0,128},{128,256},{256,384},{384,0},{1,129},{129,257},{257,385},{3... | collective-permute-start | bytes 737288 | tf_op jit(solution)/shard_map/ppermute | solution.py:50
  114.0 14.9 %collective-permute-start.12 = (f32[5,2,48,128]{3,2,1,0:T(8,128)S(1)}, f32[5,2,48,128]{3,2,1,0:T(8,128)S(1)}, u32[]{:S(2)}, u32[]{:S(2)}) collective-permute-start(f32[5,2,48,128]{3,2,1,0:T(8,128)S(1)} %collective-permute-done.11), channel_id=1, source_target_pairs={{0,384},{128,0},{256,128},{384,256},{1,385},{129,1},{257,129},{385... | collective-permute-start | bytes 737288 | tf_op jit(solution)/shard_map/ppermute | solution.py:50
  116.6 12.3 %copy-start.6 = (f32[5,16,48,128]{3,2,1,0:T(8,128)S(1)}, f32[5,16,48,128]{3,2,1,0:T(8,128)}, u32[]{:S(2)}) copy-start(f32[5,16,48,128]{3,2,1,0:T(8,128)} %constant_dynamic-update-slice_fusion.13) | copy-start | bytes 5898244
  130.3 21.0 %collective-permute-start.13 = (f32[5,9,48,128]{3,2,1,0:T(8,128)}, f32[5,9,48,128]{3,2,1,0:T(8,128)S(1)}, u32[]{:S(2)}, u32[]{:S(2)}) collective-permute-start(f32[5,9,48,128]{3,2,1,0:T(8,128)} %pad_maximum_fusion.6), channel_id=1, source_target_pairs={{504,0},{0,8},{8,16},{16,24},{24,32},{32,40},{40,48},{48,56},{56,6... | collective-permute-start | bytes 3317768 | tf_op jit(solution)/shard_map/ppermute | solution.py:17
  133.1 18.2 %collective-permute-start.14 = (f32[5,5,48,128]{3,2,1,0:T(8,128)}, f32[5,5,48,128]{3,2,1,0:T(8,128)}, u32[]{:S(2)}, u32[]{:S(2)}) collective-permute-start(f32[5,5,48,128]{3,2,1,0:T(8,128)} %constant_dynamic-slice_fusion.5), channel_id=1, source_target_pairs={{8,0},{16,8},{24,16},{32,24},{40,32},{48,40},{56,48},{64,56},{72,6... | collective-permute-start | bytes 1843208 | tf_op jit(solution)/shard_map/ppermute | solution.py:17
  156.5 19.1 %collective-permute-start.17 = (f32[3,16,1,128]{3,2,1,0:T(1,128)S(1)}, f32[3,16,1,128]{3,2,1,0:T(1,128)S(1)}, u32[]{:S(2)}, u32[]{:S(2)}) collective-permute-start(f32[3,16,1,128]{3,2,1,0:T(1,128)S(1)} %get-tuple-element.19), channel_id=1, source_target_pairs={{0,1},{1,2},{2,3},{3,4},{4,5},{5,6},{6,7},{8,9},{9,10},{10,11},{11... | collective-permute-start | bytes 73736 | tf_op jit(solution)/shard_map/ppermute | solution.py:27
  171.4 11.7 %collective-permute-start.16 = (f32[3,16,1,128]{3,2,1,0:T(1,128)S(1)}, f32[3,16,1,128]{3,2,1,0:T(1,128)S(1)}, u32[]{:S(2)}, u32[]{:S(2)}) collective-permute-start(f32[3,16,1,128]{3,2,1,0:T(1,128)S(1)} %get-tuple-element.18), channel_id=1, source_target_pairs={{1,0},{2,1},{3,2},{4,3},{5,4},{6,5},{7,6},{9,8},{10,9},{11,10},{12... | collective-permute-start | bytes 73736 | tf_op jit(solution)/shard_map/ppermute | solution.py:30
  (5 other events, 12.4 us)
